TPU v7x, 512 devices: a whole 4x4x16 slice. The times are simulated.
512 devices in a mesh: chol: 32 (over y, z_hi, x), pair: 16 (over z_lo, core).
Axes of the slice: x: 4, y: 4, z: 16 (z_hi: 2, z_lo: 8; z = z_hi * 8 + z_lo), core: 2. Of those that a mesh axis runs over, the one named last changes fastest.
Arguments:
- rotated: float32 [16384, 32768], P('chol', 'pair'), may hold values from -0.03125 to 0.03125
- green: float32 [1024, 32768], P('chol', 'pair'), may hold values from -6 to 6
- aux_field: float32 [1024, 16384], P('pair', 'chol'), may hold values from -6 to 6
Outputs:
- shifted: float32 [1024, 16384], P('pair', 'chol')
All inputs are finite; a program needn't handle non-finite values.
Results may differ from a plain program's by a relative error of at most 0.000056.
Values sent between devices are 32-bit elements; how exact they have to be, the bound alone decides.
No kernel may reach another device: no remote copies, remote signals or barrier semaphores. Data moves between devices by JAX's collectives and lax.ppermute only.
A program may use at most 64 MiB of HBM per device.

v0:
```python
import jax
import jax.numpy as jnp
from jax import lax
from jax.sharding import PartitionSpec as P

bias_cap = 1.5


def contract(rows, rotated):
    return lax.dot_general(
        rows,
        rotated,
        (((1,), (1,)), ((), ())),
        precision=lax.Precision.HIGHEST,
        preferred_element_type=jnp.float32,
    )


def body(rotated, green, aux_field):
    own_rows = aux_field.shape[0]
    gathered = contract(lax.all_gather(green, "chol", axis=0, tiled=True), rotated)
    total = lax.psum(gathered, "pair")
    share = lax.dynamic_slice_in_dim(total, lax.axis_index("pair") * own_rows, own_rows, 0)
    capped = jnp.clip(share, -bias_cap, bias_cap)
    return aux_field - capped


def solution(mesh):
    placed = (P("chol", "pair"), P("chol", "pair"), P("pair", "chol"))
    return jax.shard_map(
        body, mesh=mesh, in_specs=placed, out_specs=P("pair", "chol"), check_vma=False
    )
```

profile of v0, /device:TPU:1, one launch (start us, length us, event | category | flops | bytes accessed | tf_op | source)
XLA Modules:
  0.0 491.7 jit_solution(11579798569337451576)
XLA Ops:
  6.5 0.0 all-gather.2.cloned.1.call-start
  6.5 0.7 all-gather.2.cloned.1.call-update
  7.3 0.0 copy-start
  7.3 0.0 all-reduce.2.cloned.1.call-start
  7.3 248.5 %all-gather.2.cloned.1.call-done = f32[1024,2048]{1,0:T(8,128)} async-done(((f32[32,2048]{1,0:T(8,128)}), f32[1024,2048]{1,0:T(8,128)}) %all-gather.2.cloned.1.call-update) | async-done | bytes 8388624 | tf_op jit(solution)/shard_map/all_gather | solution.py:21
  255.8 17.1 %fusion = f32[1024,512]{1,0:T(8,128)} fusion(f32[1024,2048]{1,0:T(8,128)} %all-gather.2.cloned.1.call-done, f32[512,2048]{1,0:T(8,128)} %param.3), kind=kOutput, calls=%fused_computation.1 | convolution fusion | flops 12884901888 | bytes 14680064 | tf_op jit(solution)/shard_map/dot_general | solution.py:10
  272.9 0.0 all-reduce.2.cloned.1.call-update
  272.9 210.3 %all-reduce.2.cloned.1.call-done = f32[1024,512]{1,0:T(8,128)} async-done(((f32[1024,512]{1,0:T(8,128)}), f32[1024,512]{1,0:T(8,128)}) %all-reduce.2.cloned.1.call-update) | async-done | bytes 2097168 | tf_op jit(solution)/shard_map/psum | solution.py:22
  483.3 0.0 copy-done
  483.3 1.6 clamp_subtract_fusion
Async XLA Ops:
  6.5 249.2 %all-gather.2.cloned.1.call-start = ((), (), s32[]{:S(2)}) async-start(), calls=%async_computation | async-start | bytes 8650752 | tf_op jit(solution)/shard_map/all_gather | solution.py:21
  7.3 476.0 %copy-start = (f32[64,512]{1,0:T(8,128)S(1)}, f32[64,512]{1,0:T(8,128)}, u32[]{:S(2)}) copy-start(f32[64,512]{1,0:T(8,128)} %param.5) | copy-start | bytes 393220
  7.3 476.0 %all-reduce.2.cloned.1.call-start = ((), (), s32[]{:S(2)}) async-start(), calls=%async_computation.1 | async-start | bytes 4194304 | tf_op jit(solution)/shard_map/psum | solution.py:22
Sparse Core Ops, SparseCore 0:
  11.7 243.9 all-gather.1
  273.0 210.1 all-reduce.1
where the time goes:
time: 492 us
  waiting for transfers between devices  460 us (93%)
  matrix products  17.1 us (3%)
  between operations  13.4 us (3%)
    all_gather x1, waiting for transfers between devices, body(): lax.all_gather(green, 'chol', axis=0, tiled=True)  248 us
    psum x1, waiting for transfers between devices, body(): total = lax.psum(gathered, 'pair')  210 us
    dot_general x1, matrix products, contract(): lax.dot_general(rows, rotated, (((1,), (1,)), ((), ())), precision=lax.Pr...  17.1 us
  transfers between devices with their start and end apart: 2, of which 2 were waited for; matrix products, arithmetic and copies ran while one was open for 0% of the time, Pallas kernels for 0%

commit v1 on v0

v1 whole, which is shorter than its diff:
```python
import jax
import jax.numpy as jnp
from jax import lax
from jax.sharding import Mesh, PartitionSpec as P

bias_cap = 1.5
CHOL = ("y", "zh", "x")
PAIR = ("zl", "core")


def contract(rows, rotated):
    return lax.dot_general(rows, rotated, (((1,), (1,)), ((), ())),
                           precision=lax.Precision.HIGHEST, preferred_element_type=jnp.float32)


def body(rotated, green, aux_field):
    ny, nx = lax.axis_size("y"), lax.axis_size("x")
    nz = lax.axis_size("zh")
    rows = green.shape[0]
    g = lax.all_gather(green, "zh", axis=0, tiled=True)
    g = lax.all_gather(g, ("y", "x"), axis=0, tiled=True)
    part = contract(g, rotated)
    nl, nc = lax.axis_size("zl"), lax.axis_size("core")
    part = part.reshape(ny, nx, nz, rows, -1).transpose(0, 2, 1, 3, 4)
    part = part.reshape(nl, nc, -1, part.shape[-1]).transpose(1, 0, 2, 3).reshape(ny * nx * nz * rows, -1)
    share = lax.psum_scatter(part, "core", scatter_dimension=0, tiled=True)
    share = lax.psum_scatter(share, "zl", scatter_dimension=0, tiled=True)
    return aux_field - jnp.clip(share, -bias_cap, bias_cap)


def solution(mesh):
    ny, nz, nx = 4, 2, 4
    devs = mesh.devices.reshape(ny, nz, nx, mesh.devices.shape[1] // 2, 2)
    fine = Mesh(devs, CHOL + PAIR)
    placed = (P(CHOL, PAIR), P(CHOL, PAIR), P(PAIR, CHOL))
    return jax.shard_map(body, mesh=fine, in_specs=placed, out_specs=P(PAIR, CHOL), check_vma=False)
```

time: 492 us -> 251 us (0.51); the launches traced: 492 us -> 246 us
  waiting for transfers between devices: 460 us -> 184 us
  blocking collectives: 0 us -> 28.6 us
    psum x1 -> x0, waiting for transfers between devices: 210 us -> none  [body(): total = lax.psum(gathered, 'pair')]
    all_gather x1, waiting for transfers between devices: 248 us -> 96.9 us  [body(): g = lax.all_gather(g, ('y', 'x'), axis=0, tiled=True)]
    reduce_scatter x0 -> x2, waiting for transfers between devices: none -> 87.1 us  [the longest x1 65.8 us: body(): share = lax.psum_scatter(share, 'zl', scatter_dimension=0, tiled=True)]
    all_gather x0 -> x1, blocking collectives: none -> 28.6 us  [body(): g = lax.all_gather(green, 'zh', axis=0, tiled=True)]
  transfers between devices with their start and end apart: 2 -> 3, of which waited for: 2 -> 3; matrix products, arithmetic and copies ran while one was open for 0% -> 0% of each run, Pallas kernels for 0% -> 0%
where the time goes in v1:
time: 251 us; the launch traced here: 246 us
  waiting for transfers between devices  184 us (73%)
  blocking collectives  28.6 us (11%)
  matrix products  16.4 us (7%)
  between operations  13.1 us (5%)
    all_gather x1, waiting for transfers between devices, body(): g = lax.all_gather(g, ('y', 'x'), axis=0, tiled=True)  96.9 us
    reduce_scatter x1, waiting for transfers between devices, body(): share = lax.psum_scatter(share, 'zl', scatter_dimension=0, tiled=True)  65.8 us
    all_gather x1, blocking collectives, body(): g = lax.all_gather(green, 'zh', axis=0, tiled=True)  28.6 us
    reduce_scatter x1, waiting for transfers between devices, body(): share = lax.psum_scatter(part, 'core', scatter_dimension=0, tiled=True)  21.3 us
    dot_general x1, matrix products, contract(): lax.dot_general(rows, rotated, (((1,), (1,)), ((), ())), precision=lax.Pr...  16.4 us
  transfers between devices with their start and end apart: 3, of which 3 were waited for; matrix products, arithmetic and copies ran while one was open for 0% of the time, Pallas kernels for 0%

profile of v1, /device:TPU:1, one launch (start us, length us, event | category | flops | bytes accessed | tf_op | source)
XLA Modules:
  0.0 245.6 jit_solution(18414989563342164462)
XLA Ops:
  6.5 0.0 all-gather.2.cloned.1.call-start
  6.5 28.6 %all_gather.6 = f32[64,2048]{1,0:T(8,128)} all-gather(f32[32,2048]{1,0:T(8,128)} %param.4), channel_id=1, replica_groups=mesh['y'=4,'zh'=2,'x'=4,'zl'=8,'core'=2] {'zh'}, dimensions={0}, use_global_device_ids=true | all-gather | bytes 786432 | tf_op jit(solution)/shard_map/all_gather | solution.py:20
  35.2 0.0 all-gather.2.cloned.1.call-update
  35.2 0.0 reduce-scatter.3.cloned.1.call-start
  35.2 96.9 %all-gather.2.cloned.1.call-done = f32[1024,2048]{1,0:T(8,128)} async-done(((f32[64,2048]{1,0:T(8,128)}), f32[1024,2048]{1,0:T(8,128)}) %all-gather.2.cloned.1.call-update) | async-done | bytes 8388624 | tf_op jit(solution)/shard_map/all_gather | solution.py:21
  132.1 16.4 %fusion = f32[1024,512]{1,0:T(8,128)S(1)} fusion(f32[1024,2048]{1,0:T(8,128)} %all-gather.2.cloned.1.call-done, f32[512,2048]{1,0:T(8,128)} %param.3), kind=kOutput, calls=%fused_computation.1 | convolution fusion | flops 12884901888 | bytes 14680064 | tf_op jit(solution)/shard_map/dot_general | solution.py:12
  148.5 0.2 copy.5
  148.7 0.0 copy-start
  148.8 1.6 copy.6
  150.3 0.0 reduce-scatter.3.cloned.1.call-update
  150.3 0.0 reduce-scatter.5.cloned.1.call-start
  150.4 21.3 %reduce-scatter.3.cloned.1.call-done = f32[512,512]{1,0:T(8,128)} async-done(((f32[1024,512]{1,0:T(8,128)}), f32[512,512]{1,0:T(8,128)}) %reduce-scatter.3.cloned.1.call-update) | async-done | bytes 1048592 | tf_op jit(solution)/shard_map/reduce_scatter | solution.py:26
  171.6 0.0 reduce-scatter.5.cloned.1.call-update
  171.7 65.8 %reduce-scatter.5.cloned.1.call-done = f32[64,512]{1,0:T(8,128)} async-done(((f32[512,512]{1,0:T(8,128)}), f32[64,512]{1,0:T(8,128)}) %reduce-scatter.5.cloned.1.call-update) | async-done | bytes 131088 | tf_op jit(solution)/shard_map/reduce_scatter | solution.py:27
  237.5 0.0 copy-done
  237.5 1.6 clamp_subtract_fusion
Async XLA Ops:
  6.5 125.6 %all-gather.2.cloned.1.call-start = ((), (), s32[]{:S(2)}) async-start(), calls=%async_computation.2 | async-start | bytes 8912896 | tf_op jit(solution)/shard_map/all_gather | solution.py:21
  35.2 136.5 %reduce-scatter.3.cloned.1.call-start = ((), (), s32[]{:S(2)}) async-start(), calls=%async_computation.3 | async-start | bytes 3145728 | tf_op jit(solution)/shard_map/reduce_scatter | solution.py:26
  148.7 88.8 %copy-start = (f32[64,512]{1,0:T(8,128)S(1)}, f32[64,512]{1,0:T(8,128)}, u32[]{:S(2)}) copy-start(f32[64,512]{1,0:T(8,128)} %param.5) | copy-start | bytes 393220
  150.3 87.2 %reduce-scatter.5.cloned.1.call-start = ((), (), s32[]{:S(2)}) async-start(), calls=%async_computation.4 | async-start | bytes 1179648 | tf_op jit(solution)/shard_map/reduce_scatter | solution.py:27
Sparse Core Ops, SparseCore 0:
  35.3 96.7 all-gather.1
  150.5 21.1 reduce-scatter.2
  174.5 62.9 reduce-scatter.4

commit v2 on v1

v2 whole, which is shorter than its diff:
```python
import jax
import jax.numpy as jnp
from jax import lax
from jax.sharding import Mesh, PartitionSpec as P

bias_cap = 1.5
CHOL = ("y", "zh", "x")
PAIR = ("zl", "core")
SPLIT = False


def contract(rows, rotated):
    return lax.dot_general(rows, rotated, (((1,), (1,)), ((), ())),
                           precision=lax.Precision.HIGHEST, preferred_element_type=jnp.float32)


def swap(v, axis, bit):
    n = lax.axis_size(axis)
    return lax.ppermute(v, axis, [(i, i ^ bit) for i in range(n)])


def halve(m, axis, bit, at):
    mine = (lax.axis_index(axis) // bit) % 2
    keep = lax.dynamic_index_in_dim(m, mine, at, keepdims=False)
    send = lax.dynamic_index_in_dim(m, 1 - mine, at, keepdims=False)
    return keep + swap(send, axis, bit)


def reduce_scatter(part, nl, nc):
    m = part.reshape(nl, nc, -1, part.shape[-1])
    m = halve(m, "core", 1, 1)
    b = 1
    while b < nl:
        m = m.reshape(m.shape[0] // 2, 2, *m.shape[1:])
        m = halve(m, "zl", b, 1)
        b *= 2
    return m[0]


def body(rotated, green, aux_field):
    ny, nx, nz = lax.axis_size("y"), lax.axis_size("x"), lax.axis_size("zh")
    nl, nc = lax.axis_size("zl"), lax.axis_size("core")
    rows = green.shape[0]
    partner = swap(green, "zh", 1)
    first = lax.axis_index("zh") == 0
    if SPLIT:
        own = contract(lax.all_gather(green, ("y", "x"), axis=0, tiled=True), rotated)
        other = contract(lax.all_gather(partner, ("y", "x"), axis=0, tiled=True), rotated)
        own = own.reshape(ny, nx, rows, -1)
        other = other.reshape(ny, nx, rows, -1)
        part = jnp.stack([jnp.where(first, own, other), jnp.where(first, other, own)], axis=1)
    else:
        g = jnp.stack([jnp.where(first, green, partner), jnp.where(first, partner, green)])
        g = lax.all_gather(g, ("y", "x"), axis=0, tiled=True)
        part = contract(g.reshape(-1, g.shape[-1]), rotated)
        part = part.reshape(ny, nx, nz, rows, -1).transpose(0, 2, 1, 3, 4)
    part = part.reshape(ny * nz * nx * rows, -1)
    share = reduce_scatter(part, nl, nc)
    return aux_field - jnp.clip(share, -bias_cap, bias_cap)


def solution(mesh):
    ny, nz, nx = 4, 2, 4
    devs = mesh.devices.reshape(ny, nz, nx, mesh.devices.shape[1] // 2, 2)
    fine = Mesh(devs, CHOL + PAIR)
    placed = (P(CHOL, PAIR), P(CHOL, PAIR), P(PAIR, CHOL))
    return jax.shard_map(body, mesh=fine, in_specs=placed, out_specs=P(PAIR, CHOL), check_vma=False)
```

time: 251 us -> 216 us (0.86); the launches traced: 246 us -> 215 us
  waiting for transfers between devices: 184 us -> 147 us
  starting transfers between devices: 0.09 us -> 33.8 us
  blocking collectives: 28.6 us -> 0 us
  other arithmetic: 1.58 us -> 4.1 us
    reduce_scatter x2 -> x0, waiting for transfers between devices: 87.1 us -> none  [the longest x1 65.8 us: body(): share = lax.psum_scatter(share, 'zl', scatter_dimension=0, tiled=True)]
    ppermute x0 -> x5, waiting for transfers between devices: none -> 42.1 us  [swap(): return lax.ppermute(v, axis, [(i, i ^ bit) for i in range(n)])]
    ppermute x0 -> x5, starting transfers between devices: none -> 33.8 us  [swap(): return lax.ppermute(v, axis, [(i, i ^ bit) for i in range(n)])]
    all_gather x1 -> x0, blocking collectives: 28.6 us -> none  [body(): g = lax.all_gather(green, 'zh', axis=0, tiled=True)]
    all_gather x1, waiting for transfers between devices: 96.9 us -> 105 us  [body(): g = lax.all_gather(g, ('y', 'x'), axis=0, tiled=True)]
  transfers between devices with their start and end apart: 3 -> 6, of which waited for: 3 -> 6; matrix products, arithmetic and copies ran while one was open for 0% -> 0% of each run, Pallas kernels for 0% -> 0%
where the time goes in v2:
time: 216 us; the launch traced here: 215 us
  waiting for transfers between devices  147 us (68%)
  starting transfers between devices  33.8 us (16%)
  matrix products  16.4 us (8%)
  between operations  13.6 us (6%)
  other arithmetic  4.1 us (2%)
    all_gather x1, waiting for transfers between devices, body(): g = lax.all_gather(g, ('y', 'x'), axis=0, tiled=True)  105 us
    ppermute x5, waiting for transfers between devices, swap(): return lax.ppermute(v, axis, [(i, i ^ bit) for i in range(n)])  42.1 us
    ppermute x5, starting transfers between devices, swap(): return lax.ppermute(v, axis, [(i, i ^ bit) for i in range(n)])  33.8 us
    dot_general x1, matrix products, contract(): lax.dot_general(rows, rotated, (((1,), (1,)), ((), ())), precision=lax.Pr...  16.4 us
  transfers between devices with their start and end apart: 6, of which 6 were waited for; matrix products, arithmetic and copies ran while one was open for 0% of the time, Pallas kernels for 0%

profile of v2, /device:TPU:1, one launch (start us, length us, event | category | flops | bytes accessed | tf_op | source)
XLA Modules:
  0.0 215.2 jit_solution(10417663064187059935)
XLA Ops:
  6.5 0.0 all-gather.2.cloned.1.call-start
  6.5 16.2 %collective-permute-start = (f32[32,2048]{1,0:T(8,128)}, f32[32,2048]{1,0:T(8,128)S(1)}, u32[]{:S(2)}, u32[]{:S(2)}) collective-permute-start(f32[32,2048]{1,0:T(8,128)} %param.4), channel_id=1, source_target_pairs={{0,64},{64,0},{1,65},{65,1},{2,66},{66,2},{3,67},{67,3},{4,68},{68... | collective-permute-start | bytes 786440 | tf_op jit(solution)/shard_map/ppermute | solution.py:19
  22.8 5.6 %collective-permute-done = f32[32,2048]{1,0:T(8,128)S(1)} collective-permute-done((f32[32,2048]{1,0:T(8,128)}, f32[32,2048]{1,0:T(8,128)S(1)}, u32[]{:S(2)}, u32[]{:S(2)}) %collective-permute-start) | collective-permute-done | bytes 262176 | tf_op jit(solution)/shard_map/ppermute | solution.py:19
  28.4 1.0 select_bitcast_fusion.1
  29.4 0.9 pad_maximum_fusion
  30.2 0.0 all-gather.2.cloned.1.call-update
  30.3 104.8 %all-gather.2.cloned.1.call-done = f32[32,32,2048]{2,1,0:T(8,128)} async-done(((f32[2,32,2048]{2,1,0:T(8,128)}), f32[32,32,2048]{2,1,0:T(8,128)}) %all-gather.2.cloned.1.call-update) | async-done | bytes 8388624 | tf_op jit(solution)/shard_map/all_gather | solution.py:54
  135.1 16.4 %fusion.2 = f32[4,2,4,32,512]{4,3,1,2,0:T(8,128)S(1)} fusion(f32[4,4,2,32,2048]{4,3,2,1,0:T(8,128)} %bitcast.38, f32[512,2048]{1,0:T(8,128)} %param.3), kind=kOutput, calls=%fused_computation.2 | convolution fusion | flops 12884901888 | bytes 14680064 | tf_op jit(solution)/shard_map/dot_general | solution.py:13
  151.5 0.2 copy.6
  151.6 0.1 dynamic-slice_bitcast_fusion
  151.7 0.0 copy-start
  151.7 2.9 %collective-permute-start.1 = (f32[8,64,512]{2,1,0:T(8,128)S(1)}, f32[8,64,512]{2,1,0:T(8,128)}, u32[]{:S(2)}, u32[]{:S(2)}) collective-permute-start(f32[8,64,512]{2,1,0:T(8,128)S(1)} %dynamic-slice_bitcast_fusion), channel_id=1, source_target_pairs={{0,1},{1,0},{2,3},{3,2},{4,5},{5,4},{6,7},{7,6},{8,9},{9,8},{10,11... | collective-permute-start | bytes 3145736 | tf_op jit(solution)/shard_map/ppermute | solution.py:19
  154.7 2.4 %collective-permute-done.1 = f32[8,64,512]{2,1,0:T(8,128)} collective-permute-done((f32[8,64,512]{2,1,0:T(8,128)S(1)}, f32[8,64,512]{2,1,0:T(8,128)}, u32[]{:S(2)}, u32[]{:S(2)}) %collective-permute-start.1) | collective-permute-done | bytes 1048608 | tf_op jit(solution)/shard_map/ppermute | solution.py:19
  157.0 1.4 bitcast_add_fusion
  158.5 3.2 %collective-permute-start.2 = (f32[4,64,512]{2,1,0:T(8,128)S(1)}, f32[4,64,512]{2,1,0:T(8,128)S(1)}, u32[]{:S(2)}, u32[]{:S(2)}) collective-permute-start(f32[4,64,512]{2,1,0:T(8,128)S(1)} %dynamic-slice_bitcast_fusion.1), channel_id=1, source_target_pairs={{0,2},{2,0},{4,6},{6,4},{8,10},{10,8},{12,14},{14,12},{1,3},{3,1},... | collective-permute-start | bytes 1572872 | tf_op jit(solution)/shard_map/ppermute | solution.py:19
  161.7 11.8 %collective-permute-done.2 = f32[4,64,512]{2,1,0:T(8,128)S(1)} collective-permute-done((f32[4,64,512]{2,1,0:T(8,128)S(1)}, f32[4,64,512]{2,1,0:T(8,128)S(1)}, u32[]{:S(2)}, u32[]{:S(2)}) %collective-permute-start.2) | collective-permute-done | bytes 524320 | tf_op jit(solution)/shard_map/ppermute | solution.py:19
  173.5 0.1 bitcast_add_fusion.1
  173.6 4.2 %collective-permute-start.3 = (f32[2,64,512]{2,1,0:T(8,128)S(1)}, f32[2,64,512]{2,1,0:T(8,128)S(1)}, u32[]{:S(2)}, u32[]{:S(2)}) collective-permute-start(f32[2,64,512]{2,1,0:T(8,128)S(1)} %dynamic-slice_bitcast_fusion.2), channel_id=1, source_target_pairs={{0,4},{2,6},{4,0},{6,2},{8,12},{10,14},{12,8},{14,10},{1,5},{3,7},... | collective-permute-start | bytes 786440 | tf_op jit(solution)/shard_map/ppermute | solution.py:19
  177.9 11.4 %collective-permute-done.3 = f32[2,64,512]{2,1,0:T(8,128)S(1)} collective-permute-done((f32[2,64,512]{2,1,0:T(8,128)S(1)}, f32[2,64,512]{2,1,0:T(8,128)S(1)}, u32[]{:S(2)}, u32[]{:S(2)}) %collective-permute-start.3) | collective-permute-done | bytes 262176 | tf_op jit(solution)/shard_map/ppermute | solution.py:19
  189.4 7.3 %collective-permute-start.4 = (f32[1,64,512]{2,1,0:T(8,128)S(1)}, f32[1,64,512]{2,1,0:T(8,128)S(1)}, u32[]{:S(2)}, u32[]{:S(2)}) collective-permute-start(f32[1,64,512]{2,1,0:T(8,128)S(1)} %constant_dynamic-slice_fusion), channel_id=1, source_target_pairs={{0,8},{2,10},{4,12},{6,14},{8,0},{10,2},{12,4},{14,6},{1,9},{3,11}... | collective-permute-start | bytes 393224 | tf_op jit(solution)/shard_map/ppermute | solution.py:19
  196.7 11.0 %collective-permute-done.4 = f32[1,64,512]{2,1,0:T(8,128)S(1)} collective-permute-done((f32[1,64,512]{2,1,0:T(8,128)S(1)}, f32[1,64,512]{2,1,0:T(8,128)S(1)}, u32[]{:S(2)}, u32[]{:S(2)}) %collective-permute-start.4) | collective-permute-done | bytes 131104 | tf_op jit(solution)/shard_map/ppermute | solution.py:19
  207.7 0.0 copy-done
  207.7 0.7 bitcast_subtract_fusion
  (4 shorter events, 0.1 us)
Async XLA Ops:
  6.5 128.6 %all-gather.2.cloned.1.call-start = ((), (), s32[]{:S(2)}) async-start(), calls=%async_computation | async-start | bytes 8912896 | tf_op jit(solution)/shard_map/all_gather | solution.py:54
  6.5 21.8 %collective-permute-start = (f32[32,2048]{1,0:T(8,128)}, f32[32,2048]{1,0:T(8,128)S(1)}, u32[]{:S(2)}, u32[]{:S(2)}) collective-permute-start(f32[32,2048]{1,0:T(8,128)} %param.4), channel_id=1, source_target_pairs={{0,64},{64,0},{1,65},{65,1},{2,66},{66,2},{3,67},{67,3},{4,68},{68... | collective-permute-start | bytes 786440 | tf_op jit(solution)/shard_map/ppermute | solution.py:19
  151.7 56.0 %copy-start = (f32[64,512]{1,0:T(8,128)S(1)}, f32[64,512]{1,0:T(8,128)}, u32[]{:S(2)}) copy-start(f32[64,512]{1,0:T(8,128)} %param.5) | copy-start | bytes 393220
  151.7 5.3 %collective-permute-start.1 = (f32[8,64,512]{2,1,0:T(8,128)S(1)}, f32[8,64,512]{2,1,0:T(8,128)}, u32[]{:S(2)}, u32[]{:S(2)}) collective-permute-start(f32[8,64,512]{2,1,0:T(8,128)S(1)} %dynamic-slice_bitcast_fusion), channel_id=1, source_target_pairs={{0,1},{1,0},{2,3},{3,2},{4,5},{5,4},{6,7},{7,6},{8,9},{9,8},{10,11... | collective-permute-start | bytes 3145736 | tf_op jit(solution)/shard_map/ppermute | solution.py:19
  158.5 15.0 %collective-permute-start.2 = (f32[4,64,512]{2,1,0:T(8,128)S(1)}, f32[4,64,512]{2,1,0:T(8,128)S(1)}, u32[]{:S(2)}, u32[]{:S(2)}) collective-permute-start(f32[4,64,512]{2,1,0:T(8,128)S(1)} %dynamic-slice_bitcast_fusion.1), channel_id=1, source_target_pairs={{0,2},{2,0},{4,6},{6,4},{8,10},{10,8},{12,14},{14,12},{1,3},{3,1},... | collective-permute-start | bytes 1572872 | tf_op jit(solution)/shard_map/ppermute | solution.py:19
  173.6 15.6 %collective-permute-start.3 = (f32[2,64,512]{2,1,0:T(8,128)S(1)}, f32[2,64,512]{2,1,0:T(8,128)S(1)}, u32[]{:S(2)}, u32[]{:S(2)}) collective-permute-start(f32[2,64,512]{2,1,0:T(8,128)S(1)} %dynamic-slice_bitcast_fusion.2), channel_id=1, source_target_pairs={{0,4},{2,6},{4,0},{6,2},{8,12},{10,14},{12,8},{14,10},{1,5},{3,7},... | collective-permute-start | bytes 786440 | tf_op jit(solution)/shard_map/ppermute | solution.py:19
  189.4 18.3 %collective-permute-start.4 = (f32[1,64,512]{2,1,0:T(8,128)S(1)}, f32[1,64,512]{2,1,0:T(8,128)S(1)}, u32[]{:S(2)}, u32[]{:S(2)}) collective-permute-start(f32[1,64,512]{2,1,0:T(8,128)S(1)} %constant_dynamic-slice_fusion), channel_id=1, source_target_pairs={{0,8},{2,10},{4,12},{6,14},{8,0},{10,2},{12,4},{14,6},{1,9},{3,11}... | collective-permute-start | bytes 393224 | tf_op jit(solution)/shard_map/ppermute | solution.py:19
Sparse Core Ops, SparseCore 0:
  30.4 104.6 all-gather.1

commit v3 on v2

--- a/solution.py
+++ b/solution.py
@@ -12,6 +12,28 @@
 def contract(rows, rotated):
     return lax.dot_general(rows, rotated, (((1,), (1,)), ((), ())),
                            precision=lax.Precision.HIGHEST, preferred_element_type=jnp.float32)
+
+
+def shift(v, axis, k):
+    n = lax.axis_size(axis)
+    return lax.ppermute(v, axis, [(i, (i + k) % n) for i in range(n)])
+
+
+def ring(v, axis):
+    n = lax.axis_size(axis)
+    got = {0: v}
+    f = b = v
+    for s in range(1, (n - 1) // 2 + 1):
+        f = shift(f, axis, 1)
+        got[n - s] = f
+        b = shift(b, axis, -1)
+        got[s] = b
+    if n % 2 == 0:
+        h = v.shape[-2] // 2
+        lo = shift(f[..., :h, :], axis, 1)
+        hi = shift(b[..., h:, :], axis, -1)
+        got[n // 2] = jnp.concatenate([lo, hi], axis=-2)
+    return jnp.stack([got[k] for k in range(n)])
 
 
 def swap(v, axis, bit):
@@ -43,17 +65,18 @@
     rows = green.shape[0]
     partner = swap(green, "zh", 1)
     first = lax.axis_index("zh") == 0
-    if SPLIT:
-        own = contract(lax.all_gather(green, ("y", "x"), axis=0, tiled=True), rotated)
-        other = contract(lax.all_gather(partner, ("y", "x"), axis=0, tiled=True), rotated)
-        own = own.reshape(ny, nx, rows, -1)
-        other = other.reshape(ny, nx, rows, -1)
-        part = jnp.stack([jnp.where(first, own, other), jnp.where(first, other, own)], axis=1)
-    else:
-        g = jnp.stack([jnp.where(first, green, partner), jnp.where(first, partner, green)])
-        g = lax.all_gather(g, ("y", "x"), axis=0, tiled=True)
-        part = contract(g.reshape(-1, g.shape[-1]), rotated)
-        part = part.reshape(ny, nx, nz, rows, -1).transpose(0, 2, 1, 3, 4)
+    g = jnp.stack([jnp.where(first, green, partner), jnp.where(first, partner, green)])
+    h = rows // 2
+
+    def mm(t):
+        return contract(t.reshape(-1, t.shape[-1]), rotated).reshape(t.shape[:-1] + (rotated.shape[0],))
+
+    v1 = ring(ring(g[:, :h], "x"), "y")
+    v2 = ring(ring(g[:, h:], "y"), "x")
+    o = jnp.concatenate([mm(v1), mm(v2).transpose(1, 0, 2, 3, 4)], axis=3)
+    o = jnp.roll(o, lax.axis_index("y"), axis=0)
+    o = jnp.roll(o, lax.axis_index("x"), axis=1)
+    part = o.transpose(0, 2, 1, 3, 4)
     part = part.reshape(ny * nz * nx * rows, -1)
     share = reduce_scatter(part, nl, nc)
     return aux_field - jnp.clip(share, -bias_cap, bias_cap)

time: 216 us -> 191 us (0.88)
  waiting for transfers between devices: 147 us -> 55.4 us
  starting transfers between devices: 33.8 us -> 105 us
  between operations: 13.6 us -> 0.72 us
  local copies, waits for them, and re-layouts: 0.34 us -> 4.72 us
  other arithmetic: 4.1 us -> 6.33 us
    all_gather x1 -> x0, waiting for transfers between devices: 105 us -> none  [body(): g = lax.all_gather(g, ('y', 'x'), axis=0, tiled=True)]
    ppermute x0 -> x16, starting transfers between devices: none -> 52.6 us  [shift(): return lax.ppermute(v, axis, [(i, (i + k) % n) for i in range(n)])]
    ppermute x5, starting transfers between devices: 33.8 us -> 52.8 us  [swap(): return lax.ppermute(v, axis, [(i, i ^ bit) for i in range(n)])]
    ppermute x0 -> x16, waiting for transfers between devices: none -> 10.7 us  [shift(): return lax.ppermute(v, axis, [(i, (i + k) % n) for i in range(n)])]
    slice x0 -> x8, local copies, waits for them, and re-layouts: none -> 4.15 us  [the longest x4 2.14 us: ring(): lo = shift(f[..., :h, :], axis, 1)]
    ppermute x5, waiting for transfers between devices: 42.1 us -> 44.7 us  [swap(): return lax.ppermute(v, axis, [(i, i ^ bit) for i in range(n)])]
    dot_general x1 -> x2, matrix products: 16.4 us -> 17.9 us  [contract(): lax.dot_general(rows, rotated, (((1,), (1,)), ((), ())), precision=lax.Pr...]
  transfers between devices with their start and end apart: 6 -> 21, of which waited for: 6 -> 6; matrix products, arithmetic and copies ran while one was open for 0% -> 8% of each run, Pallas kernels for 0% -> 0%
where the time goes in v3:
time: 191 us; the launch traced here: 190 us
  starting transfers between devices  105 us (55%)
  waiting for transfers between devices  55.4 us (29%)
  matrix products  17.9 us (9%)
  other arithmetic  6.33 us (3%)
  local copies, waits for them, and re-layouts  4.72 us (2%)
    ppermute x5, starting transfers between devices, swap(): return lax.ppermute(v, axis, [(i, i ^ bit) for i in range(n)])  52.8 us
    ppermute x16, starting transfers between devices, shift(): return lax.ppermute(v, axis, [(i, (i + k) % n) for i in range(n)])  52.6 us
    ppermute x5, waiting for transfers between devices, swap(): return lax.ppermute(v, axis, [(i, i ^ bit) for i in range(n)])  44.7 us
    dot_general x2, matrix products, contract(): lax.dot_general(rows, rotated, (((1,), (1,)), ((), ())), precision=lax.Pr...  17.9 us
    ppermute x16, waiting for transfers between devices, shift(): return lax.ppermute(v, axis, [(i, (i + k) % n) for i in range(n)])  10.7 us
  transfers between devices with their start and end apart: 21, of which 6 were waited for; matrix products, arithmetic and copies ran while one was open for 8% of the time, Pallas kernels for 0%

profile of v3, /device:TPU:1, one launch (start us, length us, event | category | flops | bytes accessed | tf_op | source)
XLA Modules:
  0.0 190.4 jit_solution(12263699734937593560)
XLA Ops:
  0.0 16.2 %collective-permute-start = (f32[32,2048]{1,0:T(8,128)}, f32[32,2048]{1,0:T(8,128)S(1)}, u32[]{:S(2)}, u32[]{:S(2)}) collective-permute-start(f32[32,2048]{1,0:T(8,128)} %param.4), channel_id=1, source_target_pairs={{0,64},{64,0},{1,65},{65,1},{2,66},{66,2},{3,67},{67,3},{4,68},{68... | collective-permute-start | bytes 786440 | tf_op jit(solution)/shard_map/ppermute | solution.py:41
  16.3 5.6 %collective-permute-done = f32[32,2048]{1,0:T(8,128)S(1)} collective-permute-done((f32[32,2048]{1,0:T(8,128)}, f32[32,2048]{1,0:T(8,128)S(1)}, u32[]{:S(2)}, u32[]{:S(2)}) %collective-permute-start) | collective-permute-done | bytes 262176 | tf_op jit(solution)/shard_map/ppermute | solution.py:41
  21.8 1.0 select_bitcast_fusion
  22.9 3.8 %collective-permute-start.10 = (f32[2,16,2048]{2,1,0:T(8,128)S(1)}, f32[2,16,2048]{2,1,0:T(8,128)S(1)}, u32[]{:S(2)}, u32[]{:S(2)}) collective-permute-start(f32[2,16,2048]{2,1,0:T(8,128)S(1)} %get-tuple-element.9), channel_id=1, source_target_pairs={{0,128},{128,256},{256,384},{384,0},{1,129},{129,257},{257,385},{3... | collective-permute-start | bytes 786440 | tf_op jit(solution)/shard_map/ppermute | solution.py:19
  26.7 3.4 %collective-permute-start.9 = (f32[2,16,2048]{2,1,0:T(8,128)S(1)}, f32[2,16,2048]{2,1,0:T(8,128)S(1)}, u32[]{:S(2)}, u32[]{:S(2)}) collective-permute-start(f32[2,16,2048]{2,1,0:T(8,128)S(1)} %get-tuple-element.9), channel_id=1, source_target_pairs={{0,384},{128,0},{256,128},{384,256},{1,385},{129,1},{257,129},{385... | collective-permute-start | bytes 786440 | tf_op jit(solution)/shard_map/ppermute | solution.py:19
  30.1 3.1 %collective-permute-start.2 = (f32[2,16,2048]{2,1,0:T(8,128)S(1)}, f32[2,16,2048]{2,1,0:T(8,128)S(1)}, u32[]{:S(2)}, u32[]{:S(2)}) collective-permute-start(f32[2,16,2048]{2,1,0:T(8,128)S(1)} %get-tuple-element.10), channel_id=1, source_target_pairs={{0,16},{16,32},{32,48},{48,0},{1,17},{17,33},{33,49},{49,1},{2,18}... | collective-permute-start | bytes 786440 | tf_op jit(solution)/shard_map/ppermute | solution.py:19
  33.2 3.4 %collective-permute-start.1 = (f32[2,16,2048]{2,1,0:T(8,128)S(1)}, f32[2,16,2048]{2,1,0:T(8,128)S(1)}, u32[]{:S(2)}, u32[]{:S(2)}) collective-permute-start(f32[2,16,2048]{2,1,0:T(8,128)S(1)} %get-tuple-element.10), channel_id=1, source_target_pairs={{0,48},{16,0},{32,16},{48,32},{1,49},{17,1},{33,17},{49,33},{2,50}... | collective-permute-start | bytes 786440 | tf_op jit(solution)/shard_map/ppermute | solution.py:19
  36.6 1.9 %collective-permute-start.11 = (f32[2,8,2048]{2,1,0:T(8,128)S(1)}, f32[2,8,2048]{2,1,0:T(8,128)S(1)}, u32[]{:S(2)}, u32[]{:S(2)}) collective-permute-start(f32[2,8,2048]{2,1,0:T(8,128)S(1)} %slice.46), channel_id=1, source_target_pairs={{0,128},{128,256},{256,384},{384,0},{1,129},{129,257},{257,385},{3... | collective-permute-start | bytes 393224 | tf_op jit(solution)/shard_map/ppermute | solution.py:19
  38.6 4.6 %collective-permute-start.12 = (f32[2,8,2048]{2,1,0:T(8,128)S(1)}, f32[2,8,2048]{2,1,0:T(8,128)S(1)}, u32[]{:S(2)}, u32[]{:S(2)}) collective-permute-start(f32[2,8,2048]{2,1,0:T(8,128)S(1)} %slice.47), channel_id=1, source_target_pairs={{0,384},{128,0},{256,128},{384,256},{1,385},{129,1},{257,129},{385... | collective-permute-start | bytes 393224 | tf_op jit(solution)/shard_map/ppermute | solution.py:19
  43.2 1.9 %collective-permute-start.3 = (f32[2,8,2048]{2,1,0:T(8,128)S(1)}, f32[2,8,2048]{2,1,0:T(8,128)S(1)}, u32[]{:S(2)}, u32[]{:S(2)}) collective-permute-start(f32[2,8,2048]{2,1,0:T(8,128)S(1)} %slice.42), channel_id=1, source_target_pairs={{0,16},{16,32},{32,48},{48,0},{1,17},{17,33},{33,49},{49,1},{2,18}... | collective-permute-start | bytes 393224 | tf_op jit(solution)/shard_map/ppermute | solution.py:19
  45.1 4.6 %collective-permute-start.4 = (f32[2,8,2048]{2,1,0:T(8,128)S(1)}, f32[2,8,2048]{2,1,0:T(8,128)S(1)}, u32[]{:S(2)}, u32[]{:S(2)}) collective-permute-start(f32[2,8,2048]{2,1,0:T(8,128)S(1)} %slice.43), channel_id=1, source_target_pairs={{0,48},{16,0},{32,16},{48,32},{1,49},{17,1},{33,17},{49,33},{2,50}... | collective-permute-start | bytes 393224 | tf_op jit(solution)/shard_map/ppermute | solution.py:19
  49.8 0.2 fusion.24
  50.0 1.9 %collective-permute-start.14 = (f32[4,2,16,2048]{3,2,1,0:T(8,128)S(1)}, f32[4,2,16,2048]{3,2,1,0:T(8,128)S(1)}, u32[]{:S(2)}, u32[]{:S(2)}) collective-permute-start(f32[4,2,16,2048]{3,2,1,0:T(8,128)S(1)} %get-tuple-element.6), channel_id=1, source_target_pairs={{0,16},{16,32},{32,48},{48,0},{1,17},{17,33},{33,49},{49,1},{2,18}... | collective-permute-start | bytes 3145736 | tf_op jit(solution)/shard_map/ppermute | solution.py:19
  51.9 4.6 %collective-permute-start.13 = (f32[4,2,16,2048]{3,2,1,0:T(8,128)S(1)}, f32[4,2,16,2048]{3,2,1,0:T(8,128)S(1)}, u32[]{:S(2)}, u32[]{:S(2)}) collective-permute-start(f32[4,2,16,2048]{3,2,1,0:T(8,128)S(1)} %get-tuple-element.6), channel_id=1, source_target_pairs={{0,48},{16,0},{32,16},{48,32},{1,49},{17,1},{33,17},{49,33},{2,50}... | collective-permute-start | bytes 3145736 | tf_op jit(solution)/shard_map/ppermute | solution.py:19
  56.6 0.2 fusion.25
  56.8 1.9 %collective-permute-start.6 = (f32[4,2,16,2048]{3,2,1,0:T(8,128)S(1)}, f32[4,2,16,2048]{3,2,1,0:T(8,128)}, u32[]{:S(2)}, u32[]{:S(2)}) collective-permute-start(f32[4,2,16,2048]{3,2,1,0:T(8,128)S(1)} %get-tuple-element.8), channel_id=1, source_target_pairs={{0,128},{128,256},{256,384},{384,0},{1,129},{129,257},{257,385},{3... | collective-permute-start | bytes 3145736 | tf_op jit(solution)/shard_map/ppermute | solution.py:19
  58.7 4.6 %collective-permute-start.5 = (f32[4,2,16,2048]{3,2,1,0:T(8,128)S(1)}, f32[4,2,16,2048]{3,2,1,0:T(8,128)}, u32[]{:S(2)}, u32[]{:S(2)}) collective-permute-start(f32[4,2,16,2048]{3,2,1,0:T(8,128)S(1)} %get-tuple-element.8), channel_id=1, source_target_pairs={{0,384},{128,0},{256,128},{384,256},{1,385},{129,1},{257,129},{385... | collective-permute-start | bytes 3145736 | tf_op jit(solution)/shard_map/ppermute | solution.py:19
  63.3 10.7 %collective-permute-done.14 = f32[4,2,16,2048]{3,2,1,0:T(8,128)S(1)} collective-permute-done((f32[4,2,16,2048]{3,2,1,0:T(8,128)S(1)}, f32[4,2,16,2048]{3,2,1,0:T(8,128)S(1)}, u32[]{:S(2)}, u32[]{:S(2)}) %collective-permute-start.14) | collective-permute-done | bytes 1048608 | tf_op jit(solution)/shard_map/ppermute | solution.py:19
  74.0 0.9 slice.48
  74.9 1.9 %collective-permute-start.15 = (f32[4,2,8,2048]{3,2,1,0:T(8,128)}, f32[4,2,8,2048]{3,2,1,0:T(8,128)}, u32[]{:S(2)}, u32[]{:S(2)}) collective-permute-start(f32[4,2,8,2048]{3,2,1,0:T(8,128)} %slice.48), channel_id=1, source_target_pairs={{0,16},{16,32},{32,48},{48,0},{1,17},{17,33},{33,49},{49,1},{2,18}... | collective-permute-start | bytes 1572872 | tf_op jit(solution)/shard_map/ppermute | solution.py:19
  76.9 0.9 slice.49
  77.8 0.2 copy-done.2
  78.0 4.6 %collective-permute-start.16 = (f32[4,2,8,2048]{3,2,1,0:T(8,128)}, f32[4,2,8,2048]{3,2,1,0:T(8,128)}, u32[]{:S(2)}, u32[]{:S(2)}) collective-permute-start(f32[4,2,8,2048]{3,2,1,0:T(8,128)} %slice.49), channel_id=1, source_target_pairs={{0,48},{16,0},{32,16},{48,32},{1,49},{17,1},{33,17},{49,33},{2,50}... | collective-permute-start | bytes 1572872 | tf_op jit(solution)/shard_map/ppermute | solution.py:19
  82.6 1.2 slice.44
  83.9 1.9 %collective-permute-start.7 = (f32[4,2,8,2048]{3,2,1,0:T(8,128)S(1)}, f32[4,2,8,2048]{3,2,1,0:T(8,128)S(1)}, u32[]{:S(2)}, u32[]{:S(2)}) collective-permute-start(f32[4,2,8,2048]{3,2,1,0:T(8,128)S(1)} %slice.44), channel_id=1, source_target_pairs={{0,128},{128,256},{256,384},{384,0},{1,129},{129,257},{257,385},{3... | collective-permute-start | bytes 1572872 | tf_op jit(solution)/shard_map/ppermute | solution.py:19
  85.8 1.1 slice.45
  86.9 4.6 %collective-permute-start.8 = (f32[4,2,8,2048]{3,2,1,0:T(8,128)S(1)}, f32[4,2,8,2048]{3,2,1,0:T(8,128)S(1)}, u32[]{:S(2)}, u32[]{:S(2)}) collective-permute-start(f32[4,2,8,2048]{3,2,1,0:T(8,128)S(1)} %slice.45), channel_id=1, source_target_pairs={{0,384},{128,0},{256,128},{384,256},{1,385},{129,1},{257,129},{385... | collective-permute-start | bytes 1572872 | tf_op jit(solution)/shard_map/ppermute | solution.py:19
  91.5 1.3 maximum_bitcast_fusion.1
  92.8 0.0 copy-start.5
  92.8 9.4 %fusion.17 = f32[4,4,2,16,512]{4,3,2,1,0:T(8,128)S(1)} fusion(f32[512,2048]{1,0:T(8,128)} %param.3, f32[1,4,2,16,2048]{4,3,2,1,0:T(8,128)S(1)} %bitcast.70, f32[1,4,2,16,2048]{4,3,2,1,0:T(8,128)S(1)} %maximum_bitcast_fusion.1, f32[1,4,2,16,2048]{4,3,2,1,0:T(8,128)S(1)} %bitcast.71, f32[1,4,2,16,2048]{4,3,2,1,0:T(8,128)S(1)} %get-tuple-element.5), kind=kOutput, calls=%fused_computation.24 | convolution fusion | flops 6445596672 | bytes 9437184 | tf_op jit(solution)/shard_map/dot_general | solution.py:13
  102.3 0.1 maximum_bitcast_fusion
  102.3 8.4 %fusion = f32[4,4,2,16,512]{4,3,2,1,0:T(8,128)S(1)} fusion(f32[1,4,2,16,2048]{4,3,2,1,0:T(8,128)} %bitcast.9, f32[1,4,2,16,2048]{4,3,2,1,0:T(8,128)S(1)} %maximum_bitcast_fusion, f32[1,4,2,16,2048]{4,3,2,1,0:T(8,128)} %bitcast.7, f32[1,4,2,16,2048]{4,3,2,1,0:T(8,128)S(1)} %get-tuple-element.7, f32[512,2048]{1,0:T(8,128)S(1)} %copy-done.5), kind=kOutput, calls=%fused_computation | convolution fusion | flops 6445596672 | bytes 9437184 | tf_op jit(solution)/shard_map/dot_general | solution.py:13
  110.8 0.7 fusion.15
  111.5 0.5 fusion.13
  112.0 0.2 copy.8
  112.2 0.1 dynamic-slice_bitcast_fusion
  112.3 0.0 copy-start.4
  112.3 7.8 %collective-permute-start.17 = (f32[8,64,512]{2,1,0:T(8,128)S(1)}, f32[8,64,512]{2,1,0:T(8,128)}, u32[]{:S(2)}, u32[]{:S(2)}) collective-permute-start(f32[8,64,512]{2,1,0:T(8,128)S(1)} %dynamic-slice_bitcast_fusion), channel_id=1, source_target_pairs={{0,1},{1,0},{2,3},{3,2},{4,5},{5,4},{6,7},{7,6},{8,9},{9,8},{10,11... | collective-permute-start | bytes 3145736 | tf_op jit(solution)/shard_map/ppermute | solution.py:41
  120.2 2.4 %collective-permute-done.17 = f32[8,64,512]{2,1,0:T(8,128)} collective-permute-done((f32[8,64,512]{2,1,0:T(8,128)S(1)}, f32[8,64,512]{2,1,0:T(8,128)}, u32[]{:S(2)}, u32[]{:S(2)}) %collective-permute-start.17) | collective-permute-done | bytes 1048608 | tf_op jit(solution)/shard_map/ppermute | solution.py:41
  122.5 1.4 bitcast_add_fusion
  124.0 19.5 %collective-permute-start.18 = (f32[4,64,512]{2,1,0:T(8,128)S(1)}, f32[4,64,512]{2,1,0:T(8,128)S(1)}, u32[]{:S(2)}, u32[]{:S(2)}) collective-permute-start(f32[4,64,512]{2,1,0:T(8,128)S(1)} %dynamic-slice_bitcast_fusion.1), channel_id=1, source_target_pairs={{0,2},{2,0},{4,6},{6,4},{8,10},{10,8},{12,14},{14,12},{1,3},{3,1},... | collective-permute-start | bytes 1572872 | tf_op jit(solution)/shard_map/ppermute | solution.py:41
  143.6 11.9 %collective-permute-done.18 = f32[4,64,512]{2,1,0:T(8,128)S(1)} collective-permute-done((f32[4,64,512]{2,1,0:T(8,128)S(1)}, f32[4,64,512]{2,1,0:T(8,128)S(1)}, u32[]{:S(2)}, u32[]{:S(2)}) %collective-permute-start.18) | collective-permute-done | bytes 524320 | tf_op jit(solution)/shard_map/ppermute | solution.py:41
  155.5 0.1 bitcast_add_fusion.1
  155.6 1.9 %collective-permute-start.19 = (f32[2,64,512]{2,1,0:T(8,128)S(1)}, f32[2,64,512]{2,1,0:T(8,128)S(1)}, u32[]{:S(2)}, u32[]{:S(2)}) collective-permute-start(f32[2,64,512]{2,1,0:T(8,128)S(1)} %dynamic-slice_bitcast_fusion.2), channel_id=1, source_target_pairs={{0,4},{2,6},{4,0},{6,2},{8,12},{10,14},{12,8},{14,10},{1,5},{3,7},... | collective-permute-start | bytes 786440 | tf_op jit(solution)/shard_map/ppermute | solution.py:41
  157.6 13.8 %collective-permute-done.19 = f32[2,64,512]{2,1,0:T(8,128)S(1)} collective-permute-done((f32[2,64,512]{2,1,0:T(8,128)S(1)}, f32[2,64,512]{2,1,0:T(8,128)S(1)}, u32[]{:S(2)}, u32[]{:S(2)}) %collective-permute-start.19) | collective-permute-done | bytes 262176 | tf_op jit(solution)/shard_map/ppermute | solution.py:41
  171.4 7.2 %collective-permute-start.20 = (f32[1,64,512]{2,1,0:T(8,128)S(1)}, f32[1,64,512]{2,1,0:T(8,128)S(1)}, u32[]{:S(2)}, u32[]{:S(2)}) collective-permute-start(f32[1,64,512]{2,1,0:T(8,128)S(1)} %constant_dynamic-slice_fusion), channel_id=1, source_target_pairs={{0,8},{2,10},{4,12},{6,14},{8,0},{10,2},{12,4},{14,6},{1,9},{3,11}... | collective-permute-start | bytes 393224 | tf_op jit(solution)/shard_map/ppermute | solution.py:41
  178.6 11.1 %collective-permute-done.20 = f32[1,64,512]{2,1,0:T(8,128)S(1)} collective-permute-done((f32[1,64,512]{2,1,0:T(8,128)S(1)}, f32[1,64,512]{2,1,0:T(8,128)S(1)}, u32[]{:S(2)}, u32[]{:S(2)}) %collective-permute-start.20) | collective-permute-done | bytes 131104 | tf_op jit(solution)/shard_map/ppermute | solution.py:41
  189.7 0.7 bitcast_subtract_fusion
  (35 shorter events, 0.3 us)
Async XLA Ops:
  0.0 21.8 %collective-permute-start = (f32[32,2048]{1,0:T(8,128)}, f32[32,2048]{1,0:T(8,128)S(1)}, u32[]{:S(2)}, u32[]{:S(2)}) collective-permute-start(f32[32,2048]{1,0:T(8,128)} %param.4), channel_id=1, source_target_pairs={{0,64},{64,0},{1,65},{65,1},{2,66},{66,2},{3,67},{67,3},{4,68},{68... | collective-permute-start | bytes 786440 | tf_op jit(solution)/shard_map/ppermute | solution.py:41
  22.9 13.7 %collective-permute-start.10 = (f32[2,16,2048]{2,1,0:T(8,128)S(1)}, f32[2,16,2048]{2,1,0:T(8,128)S(1)}, u32[]{:S(2)}, u32[]{:S(2)}) collective-permute-start(f32[2,16,2048]{2,1,0:T(8,128)S(1)} %get-tuple-element.9), channel_id=1, source_target_pairs={{0,128},{128,256},{256,384},{384,0},{1,129},{129,257},{257,385},{3... | collective-permute-start | bytes 786440 | tf_op jit(solution)/shard_map/ppermute | solution.py:19
  26.7 11.8 %collective-permute-start.9 = (f32[2,16,2048]{2,1,0:T(8,128)S(1)}, f32[2,16,2048]{2,1,0:T(8,128)S(1)}, u32[]{:S(2)}, u32[]{:S(2)}) collective-permute-start(f32[2,16,2048]{2,1,0:T(8,128)S(1)} %get-tuple-element.9), channel_id=1, source_target_pairs={{0,384},{128,0},{256,128},{384,256},{1,385},{129,1},{257,129},{385... | collective-permute-start | bytes 786440 | tf_op jit(solution)/shard_map/ppermute | solution.py:19
  30.1 13.1 %collective-permute-start.2 = (f32[2,16,2048]{2,1,0:T(8,128)S(1)}, f32[2,16,2048]{2,1,0:T(8,128)S(1)}, u32[]{:S(2)}, u32[]{:S(2)}) collective-permute-start(f32[2,16,2048]{2,1,0:T(8,128)S(1)} %get-tuple-element.10), channel_id=1, source_target_pairs={{0,16},{16,32},{32,48},{48,0},{1,17},{17,33},{33,49},{49,1},{2,18}... | collective-permute-start | bytes 786440 | tf_op jit(solution)/shard_map/ppermute | solution.py:19
  33.2 11.9 %collective-permute-start.1 = (f32[2,16,2048]{2,1,0:T(8,128)S(1)}, f32[2,16,2048]{2,1,0:T(8,128)S(1)}, u32[]{:S(2)}, u32[]{:S(2)}) collective-permute-start(f32[2,16,2048]{2,1,0:T(8,128)S(1)} %get-tuple-element.10), channel_id=1, source_target_pairs={{0,48},{16,0},{32,16},{48,32},{1,49},{17,1},{33,17},{49,33},{2,50}... | collective-permute-start | bytes 786440 | tf_op jit(solution)/shard_map/ppermute | solution.py:19
  36.6 13.1 %collective-permute-start.11 = (f32[2,8,2048]{2,1,0:T(8,128)S(1)}, f32[2,8,2048]{2,1,0:T(8,128)S(1)}, u32[]{:S(2)}, u32[]{:S(2)}) collective-permute-start(f32[2,8,2048]{2,1,0:T(8,128)S(1)} %slice.46), channel_id=1, source_target_pairs={{0,128},{128,256},{256,384},{384,0},{1,129},{129,257},{257,385},{3... | collective-permute-start | bytes 393224 | tf_op jit(solution)/shard_map/ppermute | solution.py:19
  38.6 11.2 %collective-permute-start.12 = (f32[2,8,2048]{2,1,0:T(8,128)S(1)}, f32[2,8,2048]{2,1,0:T(8,128)S(1)}, u32[]{:S(2)}, u32[]{:S(2)}) collective-permute-start(f32[2,8,2048]{2,1,0:T(8,128)S(1)} %slice.47), channel_id=1, source_target_pairs={{0,384},{128,0},{256,128},{384,256},{1,385},{129,1},{257,129},{385... | collective-permute-start | bytes 393224 | tf_op jit(solution)/shard_map/ppermute | solution.py:19
  43.2 13.3 %collective-permute-start.3 = (f32[2,8,2048]{2,1,0:T(8,128)S(1)}, f32[2,8,2048]{2,1,0:T(8,128)S(1)}, u32[]{:S(2)}, u32[]{:S(2)}) collective-permute-start(f32[2,8,2048]{2,1,0:T(8,128)S(1)} %slice.42), channel_id=1, source_target_pairs={{0,16},{16,32},{32,48},{48,0},{1,17},{17,33},{33,49},{49,1},{2,18}... | collective-permute-start | bytes 393224 | tf_op jit(solution)/shard_map/ppermute | solution.py:19
  45.1 11.4 %collective-permute-start.4 = (f32[2,8,2048]{2,1,0:T(8,128)S(1)}, f32[2,8,2048]{2,1,0:T(8,128)S(1)}, u32[]{:S(2)}, u32[]{:S(2)}) collective-permute-start(f32[2,8,2048]{2,1,0:T(8,128)S(1)} %slice.43), channel_id=1, source_target_pairs={{0,48},{16,0},{32,16},{48,32},{1,49},{17,1},{33,17},{49,33},{2,50}... | collective-permute-start | bytes 393224 | tf_op jit(solution)/shard_map/ppermute | solution.py:19
  50.0 24.0 %collective-permute-start.14 = (f32[4,2,16,2048]{3,2,1,0:T(8,128)S(1)}, f32[4,2,16,2048]{3,2,1,0:T(8,128)S(1)}, u32[]{:S(2)}, u32[]{:S(2)}) collective-permute-start(f32[4,2,16,2048]{3,2,1,0:T(8,128)S(1)} %get-tuple-element.6), channel_id=1, source_target_pairs={{0,16},{16,32},{32,48},{48,0},{1,17},{17,33},{33,49},{49,1},{2,18}... | collective-permute-start | bytes 3145736 | tf_op jit(solution)/shard_map/ppermute | solution.py:19
  51.9 24.9 %collective-permute-start.13 = (f32[4,2,16,2048]{3,2,1,0:T(8,128)S(1)}, f32[4,2,16,2048]{3,2,1,0:T(8,128)S(1)}, u32[]{:S(2)}, u32[]{:S(2)}) collective-permute-start(f32[4,2,16,2048]{3,2,1,0:T(8,128)S(1)} %get-tuple-element.6), channel_id=1, source_target_pairs={{0,48},{16,0},{32,16},{48,32},{1,49},{17,1},{33,17},{49,33},{2,50}... | collective-permute-start | bytes 3145736 | tf_op jit(solution)/shard_map/ppermute | solution.py:19
  56.8 25.8 %collective-permute-start.6 = (f32[4,2,16,2048]{3,2,1,0:T(8,128)S(1)}, f32[4,2,16,2048]{3,2,1,0:T(8,128)}, u32[]{:S(2)}, u32[]{:S(2)}) collective-permute-start(f32[4,2,16,2048]{3,2,1,0:T(8,128)S(1)} %get-tuple-element.8), channel_id=1, source_target_pairs={{0,128},{128,256},{256,384},{384,0},{1,129},{129,257},{257,385},{3... | collective-permute-start | bytes 3145736 | tf_op jit(solution)/shard_map/ppermute | solution.py:19
  58.7 27.0 %collective-permute-start.5 = (f32[4,2,16,2048]{3,2,1,0:T(8,128)S(1)}, f32[4,2,16,2048]{3,2,1,0:T(8,128)}, u32[]{:S(2)}, u32[]{:S(2)}) collective-permute-start(f32[4,2,16,2048]{3,2,1,0:T(8,128)S(1)} %get-tuple-element.8), channel_id=1, source_target_pairs={{0,384},{128,0},{256,128},{384,256},{1,385},{129,1},{257,129},{385... | collective-permute-start | bytes 3145736 | tf_op jit(solution)/shard_map/ppermute | solution.py:19
  74.0 2.8 %copy-start = (f32[4,2,16,2048]{3,2,1,0:T(8,128)}, f32[4,2,16,2048]{3,2,1,0:T(8,128)S(1)}, u32[]{:S(2)}) copy-start(f32[4,2,16,2048]{3,2,1,0:T(8,128)S(1)} %collective-permute-done.14) | copy-start | bytes 3145732
  74.9 16.5 %collective-permute-start.15 = (f32[4,2,8,2048]{3,2,1,0:T(8,128)}, f32[4,2,8,2048]{3,2,1,0:T(8,128)}, u32[]{:S(2)}, u32[]{:S(2)}) collective-permute-start(f32[4,2,8,2048]{3,2,1,0:T(8,128)} %slice.48), channel_id=1, source_target_pairs={{0,16},{16,32},{32,48},{48,0},{1,17},{17,33},{33,49},{49,1},{2,18}... | collective-permute-start | bytes 1572872 | tf_op jit(solution)/shard_map/ppermute | solution.py:19
  76.9 1.1 copy-start.2
  78.0 13.5 %collective-permute-start.16 = (f32[4,2,8,2048]{3,2,1,0:T(8,128)}, f32[4,2,8,2048]{3,2,1,0:T(8,128)}, u32[]{:S(2)}, u32[]{:S(2)}) collective-permute-start(f32[4,2,8,2048]{3,2,1,0:T(8,128)} %slice.49), channel_id=1, source_target_pairs={{0,48},{16,0},{32,16},{48,32},{1,49},{17,1},{33,17},{49,33},{2,50}... | collective-permute-start | bytes 1572872 | tf_op jit(solution)/shard_map/ppermute | solution.py:19
  82.6 10.2 %copy-start.1 = (f32[4,2,16,2048]{3,2,1,0:T(8,128)S(1)}, f32[4,2,16,2048]{3,2,1,0:T(8,128)}, u32[]{:S(2)}) copy-start(f32[4,2,16,2048]{3,2,1,0:T(8,128)} %copy-done) | copy-start | bytes 3145732
  82.6 10.2 %copy-start.3 = (f32[4,2,16,2048]{3,2,1,0:T(8,128)S(1)}, f32[4,2,16,2048]{3,2,1,0:T(8,128)}, u32[]{:S(2)}) copy-start(f32[4,2,16,2048]{3,2,1,0:T(8,128)} %copy-done.2) | copy-start | bytes 3145732
  83.9 18.4 %collective-permute-start.7 = (f32[4,2,8,2048]{3,2,1,0:T(8,128)S(1)}, f32[4,2,8,2048]{3,2,1,0:T(8,128)S(1)}, u32[]{:S(2)}, u32[]{:S(2)}) collective-permute-start(f32[4,2,8,2048]{3,2,1,0:T(8,128)S(1)} %slice.44), channel_id=1, source_target_pairs={{0,128},{128,256},{256,384},{384,0},{1,129},{129,257},{257,385},{3... | collective-permute-start | bytes 1572872 | tf_op jit(solution)/shard_map/ppermute | solution.py:19
  86.9 15.4 %collective-permute-start.8 = (f32[4,2,8,2048]{3,2,1,0:T(8,128)S(1)}, f32[4,2,8,2048]{3,2,1,0:T(8,128)S(1)}, u32[]{:S(2)}, u32[]{:S(2)}) collective-permute-start(f32[4,2,8,2048]{3,2,1,0:T(8,128)S(1)} %slice.45), channel_id=1, source_target_pairs={{0,384},{128,0},{256,128},{384,256},{1,385},{129,1},{257,129},{385... | collective-permute-start | bytes 1572872 | tf_op jit(solution)/shard_map/ppermute | solution.py:19
  92.8 9.5 %copy-start.5 = (f32[512,2048]{1,0:T(8,128)S(1)}, f32[512,2048]{1,0:T(8,128)}, u32[]{:S(2)}) copy-start(f32[512,2048]{1,0:T(8,128)} %param.3) | copy-start | bytes 12582916
  112.3 77.5 %copy-start.4 = (f32[64,512]{1,0:T(8,128)S(1)}, f32[64,512]{1,0:T(8,128)}, u32[]{:S(2)}) copy-start(f32[64,512]{1,0:T(8,128)} %param.5) | copy-start | bytes 393220
  112.3 10.2 %collective-permute-start.17 = (f32[8,64,512]{2,1,0:T(8,128)S(1)}, f32[8,64,512]{2,1,0:T(8,128)}, u32[]{:S(2)}, u32[]{:S(2)}) collective-permute-start(f32[8,64,512]{2,1,0:T(8,128)S(1)} %dynamic-slice_bitcast_fusion), channel_id=1, source_target_pairs={{0,1},{1,0},{2,3},{3,2},{4,5},{5,4},{6,7},{7,6},{8,9},{9,8},{10,11... | collective-permute-start | bytes 3145736 | tf_op jit(solution)/shard_map/ppermute | solution.py:41
  124.0 31.4 %collective-permute-start.18 = (f32[4,64,512]{2,1,0:T(8,128)S(1)}, f32[4,64,512]{2,1,0:T(8,128)S(1)}, u32[]{:S(2)}, u32[]{:S(2)}) collective-permute-start(f32[4,64,512]{2,1,0:T(8,128)S(1)} %dynamic-slice_bitcast_fusion.1), channel_id=1, source_target_pairs={{0,2},{2,0},{4,6},{6,4},{8,10},{10,8},{12,14},{14,12},{1,3},{3,1},... | collective-permute-start | bytes 1572872 | tf_op jit(solution)/shard_map/ppermute | solution.py:41
  155.6 15.7 %collective-permute-start.19 = (f32[2,64,512]{2,1,0:T(8,128)S(1)}, f32[2,64,512]{2,1,0:T(8,128)S(1)}, u32[]{:S(2)}, u32[]{:S(2)}) collective-permute-start(f32[2,64,512]{2,1,0:T(8,128)S(1)} %dynamic-slice_bitcast_fusion.2), channel_id=1, source_target_pairs={{0,4},{2,6},{4,0},{6,2},{8,12},{10,14},{12,8},{14,10},{1,5},{3,7},... | collective-permute-start | bytes 786440 | tf_op jit(solution)/shard_map/ppermute | solution.py:41
  171.4 18.3 %collective-permute-start.20 = (f32[1,64,512]{2,1,0:T(8,128)S(1)}, f32[1,64,512]{2,1,0:T(8,128)S(1)}, u32[]{:S(2)}, u32[]{:S(2)}) collective-permute-start(f32[1,64,512]{2,1,0:T(8,128)S(1)} %constant_dynamic-slice_fusion), channel_id=1, source_target_pairs={{0,8},{2,10},{4,12},{6,14},{8,0},{10,2},{12,4},{14,6},{1,9},{3,11}... | collective-permute-start | bytes 393224 | tf_op jit(solution)/shard_map/ppermute | solution.py:41

commit v4 on v3

--- a/solution.py
+++ b/solution.py
@@ -11,7 +11,7 @@
 
 def contract(rows, rotated):
     return lax.dot_general(rows, rotated, (((1,), (1,)), ((), ())),
-                           precision=lax.Precision.HIGHEST, preferred_element_type=jnp.float32)
+                           precision=lax.Precision.HIGH, preferred_element_type=jnp.float32)
 
 
 def shift(v, axis, k):

time: 191 us -> 184 us (0.963)
  matrix products: 17.9 us -> 10.8 us
    dot_general x2, matrix products: 17.9 us -> 10.8 us  [contract(): lax.dot_general(rows, rotated, (((1,), (1,)), ((), ())), precision=lax.Pr...]
  transfers between devices with their start and end apart: 21 -> 21, of which waited for: 6 -> 6; matrix products, arithmetic and copies ran while one was open for 8% -> 6% of each run, Pallas kernels for 0% -> 0%
where the time goes in v4:
time: 184 us; the launch traced here: 183 us
  starting transfers between devices  106 us (58%)
  waiting for transfers between devices  55.2 us (30%)
  matrix products  10.8 us (6%)
  other arithmetic  6.34 us (3%)
  local copies, waits for them, and re-layouts  4.72 us (3%)
    ppermute x5, starting transfers between devices, swap(): return lax.ppermute(v, axis, [(i, i ^ bit) for i in range(n)])  53 us
    ppermute x16, starting transfers between devices, shift(): return lax.ppermute(v, axis, [(i, (i + k) % n) for i in range(n)])  52.6 us
    ppermute x5, waiting for transfers between devices, swap(): return lax.ppermute(v, axis, [(i, i ^ bit) for i in range(n)])  44.4 us
    dot_general x2, matrix products, contract(): lax.dot_general(rows, rotated, (((1,), (1,)), ((), ())), precision=lax.Pr...  10.8 us
    ppermute x16, waiting for transfers between devices, shift(): return lax.ppermute(v, axis, [(i, (i + k) % n) for i in range(n)])  10.7 us
  transfers between devices with their start and end apart: 21, of which 6 were waited for; matrix products, arithmetic and copies ran while one was open for 6% of the time, Pallas kernels for 0%

profile of v4, /device:TPU:1, one launch (start us, length us, event | category | flops | bytes accessed | tf_op | source)
XLA Modules:
  0.0 183.4 jit_solution(14388585499579113958)
XLA Ops:
  0.0 16.2 %collective-permute-start = (f32[32,2048]{1,0:T(8,128)}, f32[32,2048]{1,0:T(8,128)S(1)}, u32[]{:S(2)}, u32[]{:S(2)}) collective-permute-start(f32[32,2048]{1,0:T(8,128)} %param.4), channel_id=1, source_target_pairs={{0,64},{64,0},{1,65},{65,1},{2,66},{66,2},{3,67},{67,3},{4,68},{68... | collective-permute-start | bytes 786440 | tf_op jit(solution)/shard_map/ppermute | solution.py:41
  16.3 5.6 %collective-permute-done = f32[32,2048]{1,0:T(8,128)S(1)} collective-permute-done((f32[32,2048]{1,0:T(8,128)}, f32[32,2048]{1,0:T(8,128)S(1)}, u32[]{:S(2)}, u32[]{:S(2)}) %collective-permute-start) | collective-permute-done | bytes 262176 | tf_op jit(solution)/shard_map/ppermute | solution.py:41
  21.8 1.0 select_bitcast_fusion
  22.9 3.8 %collective-permute-start.10 = (f32[2,16,2048]{2,1,0:T(8,128)S(1)}, f32[2,16,2048]{2,1,0:T(8,128)S(1)}, u32[]{:S(2)}, u32[]{:S(2)}) collective-permute-start(f32[2,16,2048]{2,1,0:T(8,128)S(1)} %get-tuple-element.9), channel_id=1, source_target_pairs={{0,128},{128,256},{256,384},{384,0},{1,129},{129,257},{257,385},{3... | collective-permute-start | bytes 786440 | tf_op jit(solution)/shard_map/ppermute | solution.py:19
  26.7 3.4 %collective-permute-start.9 = (f32[2,16,2048]{2,1,0:T(8,128)S(1)}, f32[2,16,2048]{2,1,0:T(8,128)S(1)}, u32[]{:S(2)}, u32[]{:S(2)}) collective-permute-start(f32[2,16,2048]{2,1,0:T(8,128)S(1)} %get-tuple-element.9), channel_id=1, source_target_pairs={{0,384},{128,0},{256,128},{384,256},{1,385},{129,1},{257,129},{385... | collective-permute-start | bytes 786440 | tf_op jit(solution)/shard_map/ppermute | solution.py:19
  30.1 3.1 %collective-permute-start.2 = (f32[2,16,2048]{2,1,0:T(8,128)S(1)}, f32[2,16,2048]{2,1,0:T(8,128)S(1)}, u32[]{:S(2)}, u32[]{:S(2)}) collective-permute-start(f32[2,16,2048]{2,1,0:T(8,128)S(1)} %get-tuple-element.10), channel_id=1, source_target_pairs={{0,16},{16,32},{32,48},{48,0},{1,17},{17,33},{33,49},{49,1},{2,18}... | collective-permute-start | bytes 786440 | tf_op jit(solution)/shard_map/ppermute | solution.py:19
  33.2 3.4 %collective-permute-start.1 = (f32[2,16,2048]{2,1,0:T(8,128)S(1)}, f32[2,16,2048]{2,1,0:T(8,128)S(1)}, u32[]{:S(2)}, u32[]{:S(2)}) collective-permute-start(f32[2,16,2048]{2,1,0:T(8,128)S(1)} %get-tuple-element.10), channel_id=1, source_target_pairs={{0,48},{16,0},{32,16},{48,32},{1,49},{17,1},{33,17},{49,33},{2,50}... | collective-permute-start | bytes 786440 | tf_op jit(solution)/shard_map/ppermute | solution.py:19
  36.6 1.9 %collective-permute-start.11 = (f32[2,8,2048]{2,1,0:T(8,128)S(1)}, f32[2,8,2048]{2,1,0:T(8,128)S(1)}, u32[]{:S(2)}, u32[]{:S(2)}) collective-permute-start(f32[2,8,2048]{2,1,0:T(8,128)S(1)} %slice.46), channel_id=1, source_target_pairs={{0,128},{128,256},{256,384},{384,0},{1,129},{129,257},{257,385},{3... | collective-permute-start | bytes 393224 | tf_op jit(solution)/shard_map/ppermute | solution.py:19
  38.6 4.6 %collective-permute-start.12 = (f32[2,8,2048]{2,1,0:T(8,128)S(1)}, f32[2,8,2048]{2,1,0:T(8,128)S(1)}, u32[]{:S(2)}, u32[]{:S(2)}) collective-permute-start(f32[2,8,2048]{2,1,0:T(8,128)S(1)} %slice.47), channel_id=1, source_target_pairs={{0,384},{128,0},{256,128},{384,256},{1,385},{129,1},{257,129},{385... | collective-permute-start | bytes 393224 | tf_op jit(solution)/shard_map/ppermute | solution.py:19
  43.2 1.9 %collective-permute-start.3 = (f32[2,8,2048]{2,1,0:T(8,128)S(1)}, f32[2,8,2048]{2,1,0:T(8,128)S(1)}, u32[]{:S(2)}, u32[]{:S(2)}) collective-permute-start(f32[2,8,2048]{2,1,0:T(8,128)S(1)} %slice.42), channel_id=1, source_target_pairs={{0,16},{16,32},{32,48},{48,0},{1,17},{17,33},{33,49},{49,1},{2,18}... | collective-permute-start | bytes 393224 | tf_op jit(solution)/shard_map/ppermute | solution.py:19
  45.1 4.6 %collective-permute-start.4 = (f32[2,8,2048]{2,1,0:T(8,128)S(1)}, f32[2,8,2048]{2,1,0:T(8,128)S(1)}, u32[]{:S(2)}, u32[]{:S(2)}) collective-permute-start(f32[2,8,2048]{2,1,0:T(8,128)S(1)} %slice.43), channel_id=1, source_target_pairs={{0,48},{16,0},{32,16},{48,32},{1,49},{17,1},{33,17},{49,33},{2,50}... | collective-permute-start | bytes 393224 | tf_op jit(solution)/shard_map/ppermute | solution.py:19
  49.8 0.2 fusion.24
  50.0 1.9 %collective-permute-start.14 = (f32[4,2,16,2048]{3,2,1,0:T(8,128)S(1)}, f32[4,2,16,2048]{3,2,1,0:T(8,128)S(1)}, u32[]{:S(2)}, u32[]{:S(2)}) collective-permute-start(f32[4,2,16,2048]{3,2,1,0:T(8,128)S(1)} %get-tuple-element.6), channel_id=1, source_target_pairs={{0,16},{16,32},{32,48},{48,0},{1,17},{17,33},{33,49},{49,1},{2,18}... | collective-permute-start | bytes 3145736 | tf_op jit(solution)/shard_map/ppermute | solution.py:19
  51.9 4.6 %collective-permute-start.13 = (f32[4,2,16,2048]{3,2,1,0:T(8,128)S(1)}, f32[4,2,16,2048]{3,2,1,0:T(8,128)S(1)}, u32[]{:S(2)}, u32[]{:S(2)}) collective-permute-start(f32[4,2,16,2048]{3,2,1,0:T(8,128)S(1)} %get-tuple-element.6), channel_id=1, source_target_pairs={{0,48},{16,0},{32,16},{48,32},{1,49},{17,1},{33,17},{49,33},{2,50}... | collective-permute-start | bytes 3145736 | tf_op jit(solution)/shard_map/ppermute | solution.py:19
  56.6 0.2 fusion.25
  56.8 1.9 %collective-permute-start.6 = (f32[4,2,16,2048]{3,2,1,0:T(8,128)S(1)}, f32[4,2,16,2048]{3,2,1,0:T(8,128)}, u32[]{:S(2)}, u32[]{:S(2)}) collective-permute-start(f32[4,2,16,2048]{3,2,1,0:T(8,128)S(1)} %get-tuple-element.8), channel_id=1, source_target_pairs={{0,128},{128,256},{256,384},{384,0},{1,129},{129,257},{257,385},{3... | collective-permute-start | bytes 3145736 | tf_op jit(solution)/shard_map/ppermute | solution.py:19
  58.7 4.6 %collective-permute-start.5 = (f32[4,2,16,2048]{3,2,1,0:T(8,128)S(1)}, f32[4,2,16,2048]{3,2,1,0:T(8,128)}, u32[]{:S(2)}, u32[]{:S(2)}) collective-permute-start(f32[4,2,16,2048]{3,2,1,0:T(8,128)S(1)} %get-tuple-element.8), channel_id=1, source_target_pairs={{0,384},{128,0},{256,128},{384,256},{1,385},{129,1},{257,129},{385... | collective-permute-start | bytes 3145736 | tf_op jit(solution)/shard_map/ppermute | solution.py:19
  63.3 10.7 %collective-permute-done.14 = f32[4,2,16,2048]{3,2,1,0:T(8,128)S(1)} collective-permute-done((f32[4,2,16,2048]{3,2,1,0:T(8,128)S(1)}, f32[4,2,16,2048]{3,2,1,0:T(8,128)S(1)}, u32[]{:S(2)}, u32[]{:S(2)}) %collective-permute-start.14) | collective-permute-done | bytes 1048608 | tf_op jit(solution)/shard_map/ppermute | solution.py:19
  74.0 0.9 slice.48
  74.9 1.9 %collective-permute-start.15 = (f32[4,2,8,2048]{3,2,1,0:T(8,128)}, f32[4,2,8,2048]{3,2,1,0:T(8,128)}, u32[]{:S(2)}, u32[]{:S(2)}) collective-permute-start(f32[4,2,8,2048]{3,2,1,0:T(8,128)} %slice.48), channel_id=1, source_target_pairs={{0,16},{16,32},{32,48},{48,0},{1,17},{17,33},{33,49},{49,1},{2,18}... | collective-permute-start | bytes 1572872 | tf_op jit(solution)/shard_map/ppermute | solution.py:19
  76.9 0.9 slice.49
  77.8 0.2 copy-done.2
  78.0 4.6 %collective-permute-start.16 = (f32[4,2,8,2048]{3,2,1,0:T(8,128)}, f32[4,2,8,2048]{3,2,1,0:T(8,128)}, u32[]{:S(2)}, u32[]{:S(2)}) collective-permute-start(f32[4,2,8,2048]{3,2,1,0:T(8,128)} %slice.49), channel_id=1, source_target_pairs={{0,48},{16,0},{32,16},{48,32},{1,49},{17,1},{33,17},{49,33},{2,50}... | collective-permute-start | bytes 1572872 | tf_op jit(solution)/shard_map/ppermute | solution.py:19
  82.6 1.2 slice.44
  83.9 1.9 %collective-permute-start.7 = (f32[4,2,8,2048]{3,2,1,0:T(8,128)S(1)}, f32[4,2,8,2048]{3,2,1,0:T(8,128)S(1)}, u32[]{:S(2)}, u32[]{:S(2)}) collective-permute-start(f32[4,2,8,2048]{3,2,1,0:T(8,128)S(1)} %slice.44), channel_id=1, source_target_pairs={{0,128},{128,256},{256,384},{384,0},{1,129},{129,257},{257,385},{3... | collective-permute-start | bytes 1572872 | tf_op jit(solution)/shard_map/ppermute | solution.py:19
  85.8 1.1 slice.45
  86.9 4.6 %collective-permute-start.8 = (f32[4,2,8,2048]{3,2,1,0:T(8,128)S(1)}, f32[4,2,8,2048]{3,2,1,0:T(8,128)S(1)}, u32[]{:S(2)}, u32[]{:S(2)}) collective-permute-start(f32[4,2,8,2048]{3,2,1,0:T(8,128)S(1)} %slice.45), channel_id=1, source_target_pairs={{0,384},{128,0},{256,128},{384,256},{1,385},{129,1},{257,129},{385... | collective-permute-start | bytes 1572872 | tf_op jit(solution)/shard_map/ppermute | solution.py:19
  91.5 1.3 maximum_bitcast_fusion.1
  92.8 0.0 copy-start.5
  92.8 5.8 %fusion.17 = f32[4,4,2,16,512]{4,3,2,1,0:T(8,128)S(1)} fusion(f32[512,2048]{1,0:T(8,128)} %param.3, f32[1,4,2,16,2048]{4,3,2,1,0:T(8,128)S(1)} %bitcast.70, f32[1,4,2,16,2048]{4,3,2,1,0:T(8,128)S(1)} %maximum_bitcast_fusion.1, f32[1,4,2,16,2048]{4,3,2,1,0:T(8,128)S(1)} %bitcast.71, f32[1,4,2,16,2048]{4,3,2,1,0:T(8,128)S(1)} %get-tuple-element.5), kind=kOutput, calls=%fused_computation.24 | convolution fusion | flops 3224371200 | bytes 9437184 | tf_op jit(solution)/shard_map/dot_general | solution.py:13
  98.6 0.1 maximum_bitcast_fusion
  98.7 5.0 %fusion = f32[4,4,2,16,512]{4,3,2,1,0:T(8,128)S(1)} fusion(f32[1,4,2,16,2048]{4,3,2,1,0:T(8,128)} %bitcast.9, f32[1,4,2,16,2048]{4,3,2,1,0:T(8,128)S(1)} %maximum_bitcast_fusion, f32[1,4,2,16,2048]{4,3,2,1,0:T(8,128)} %bitcast.7, f32[1,4,2,16,2048]{4,3,2,1,0:T(8,128)S(1)} %get-tuple-element.7, f32[512,2048]{1,0:T(8,128)S(1)} %copy-done.5), kind=kOutput, calls=%fused_computation | convolution fusion | flops 3224371200 | bytes 9437184 | tf_op jit(solution)/shard_map/dot_general | solution.py:13
  103.7 0.7 fusion.15
  104.4 0.5 fusion.13
  105.0 0.2 copy.8
  105.1 0.1 dynamic-slice_bitcast_fusion
  105.2 0.0 copy-start.4
  105.2 7.8 %collective-permute-start.17 = (f32[8,64,512]{2,1,0:T(8,128)S(1)}, f32[8,64,512]{2,1,0:T(8,128)}, u32[]{:S(2)}, u32[]{:S(2)}) collective-permute-start(f32[8,64,512]{2,1,0:T(8,128)S(1)} %dynamic-slice_bitcast_fusion), channel_id=1, source_target_pairs={{0,1},{1,0},{2,3},{3,2},{4,5},{5,4},{6,7},{7,6},{8,9},{9,8},{10,11... | collective-permute-start | bytes 3145736 | tf_op jit(solution)/shard_map/ppermute | solution.py:41
  113.1 2.4 %collective-permute-done.17 = f32[8,64,512]{2,1,0:T(8,128)} collective-permute-done((f32[8,64,512]{2,1,0:T(8,128)S(1)}, f32[8,64,512]{2,1,0:T(8,128)}, u32[]{:S(2)}, u32[]{:S(2)}) %collective-permute-start.17) | collective-permute-done | bytes 1048608 | tf_op jit(solution)/shard_map/ppermute | solution.py:41
  115.5 1.4 bitcast_add_fusion
  117.0 19.5 %collective-permute-start.18 = (f32[4,64,512]{2,1,0:T(8,128)S(1)}, f32[4,64,512]{2,1,0:T(8,128)S(1)}, u32[]{:S(2)}, u32[]{:S(2)}) collective-permute-start(f32[4,64,512]{2,1,0:T(8,128)S(1)} %dynamic-slice_bitcast_fusion.1), channel_id=1, source_target_pairs={{0,2},{2,0},{4,6},{6,4},{8,10},{10,8},{12,14},{14,12},{1,3},{3,1},... | collective-permute-start | bytes 1572872 | tf_op jit(solution)/shard_map/ppermute | solution.py:41
  136.5 11.9 %collective-permute-done.18 = f32[4,64,512]{2,1,0:T(8,128)S(1)} collective-permute-done((f32[4,64,512]{2,1,0:T(8,128)S(1)}, f32[4,64,512]{2,1,0:T(8,128)S(1)}, u32[]{:S(2)}, u32[]{:S(2)}) %collective-permute-start.18) | collective-permute-done | bytes 524320 | tf_op jit(solution)/shard_map/ppermute | solution.py:41
  148.4 0.1 bitcast_add_fusion.1
  148.5 1.9 %collective-permute-start.19 = (f32[2,64,512]{2,1,0:T(8,128)S(1)}, f32[2,64,512]{2,1,0:T(8,128)S(1)}, u32[]{:S(2)}, u32[]{:S(2)}) collective-permute-start(f32[2,64,512]{2,1,0:T(8,128)S(1)} %dynamic-slice_bitcast_fusion.2), channel_id=1, source_target_pairs={{0,4},{2,6},{4,0},{6,2},{8,12},{10,14},{12,8},{14,10},{1,5},{3,7},... | collective-permute-start | bytes 786440 | tf_op jit(solution)/shard_map/ppermute | solution.py:41
  150.5 13.8 %collective-permute-done.19 = f32[2,64,512]{2,1,0:T(8,128)S(1)} collective-permute-done((f32[2,64,512]{2,1,0:T(8,128)S(1)}, f32[2,64,512]{2,1,0:T(8,128)S(1)}, u32[]{:S(2)}, u32[]{:S(2)}) %collective-permute-start.19) | collective-permute-done | bytes 262176 | tf_op jit(solution)/shard_map/ppermute | solution.py:41
  164.3 7.5 %collective-permute-start.20 = (f32[1,64,512]{2,1,0:T(8,128)S(1)}, f32[1,64,512]{2,1,0:T(8,128)S(1)}, u32[]{:S(2)}, u32[]{:S(2)}) collective-permute-start(f32[1,64,512]{2,1,0:T(8,128)S(1)} %constant_dynamic-slice_fusion), channel_id=1, source_target_pairs={{0,8},{2,10},{4,12},{6,14},{8,0},{10,2},{12,4},{14,6},{1,9},{3,11}... | collective-permute-start | bytes 393224 | tf_op jit(solution)/shard_map/ppermute | solution.py:41
  171.8 10.9 %collective-permute-done.20 = f32[1,64,512]{2,1,0:T(8,128)S(1)} collective-permute-done((f32[1,64,512]{2,1,0:T(8,128)S(1)}, f32[1,64,512]{2,1,0:T(8,128)S(1)}, u32[]{:S(2)}, u32[]{:S(2)}) %collective-permute-start.20) | collective-permute-done | bytes 131104 | tf_op jit(solution)/shard_map/ppermute | solution.py:41
  182.7 0.7 bitcast_subtract_fusion
  (35 shorter events, 0.3 us)
Async XLA Ops:
  0.0 21.8 %collective-permute-start = (f32[32,2048]{1,0:T(8,128)}, f32[32,2048]{1,0:T(8,128)S(1)}, u32[]{:S(2)}, u32[]{:S(2)}) collective-permute-start(f32[32,2048]{1,0:T(8,128)} %param.4), channel_id=1, source_target_pairs={{0,64},{64,0},{1,65},{65,1},{2,66},{66,2},{3,67},{67,3},{4,68},{68... | collective-permute-start | bytes 786440 | tf_op jit(solution)/shard_map/ppermute | solution.py:41
  22.9 13.7 %collective-permute-start.10 = (f32[2,16,2048]{2,1,0:T(8,128)S(1)}, f32[2,16,2048]{2,1,0:T(8,128)S(1)}, u32[]{:S(2)}, u32[]{:S(2)}) collective-permute-start(f32[2,16,2048]{2,1,0:T(8,128)S(1)} %get-tuple-element.9), channel_id=1, source_target_pairs={{0,128},{128,256},{256,384},{384,0},{1,129},{129,257},{257,385},{3... | collective-permute-start | bytes 786440 | tf_op jit(solution)/shard_map/ppermute | solution.py:19
  26.7 11.8 %collective-permute-start.9 = (f32[2,16,2048]{2,1,0:T(8,128)S(1)}, f32[2,16,2048]{2,1,0:T(8,128)S(1)}, u32[]{:S(2)}, u32[]{:S(2)}) collective-permute-start(f32[2,16,2048]{2,1,0:T(8,128)S(1)} %get-tuple-element.9), channel_id=1, source_target_pairs={{0,384},{128,0},{256,128},{384,256},{1,385},{129,1},{257,129},{385... | collective-permute-start | bytes 786440 | tf_op jit(solution)/shard_map/ppermute | solution.py:19
  30.1 13.1 %collective-permute-start.2 = (f32[2,16,2048]{2,1,0:T(8,128)S(1)}, f32[2,16,2048]{2,1,0:T(8,128)S(1)}, u32[]{:S(2)}, u32[]{:S(2)}) collective-permute-start(f32[2,16,2048]{2,1,0:T(8,128)S(1)} %get-tuple-element.10), channel_id=1, source_target_pairs={{0,16},{16,32},{32,48},{48,0},{1,17},{17,33},{33,49},{49,1},{2,18}... | collective-permute-start | bytes 786440 | tf_op jit(solution)/shard_map/ppermute | solution.py:19
  33.2 11.9 %collective-permute-start.1 = (f32[2,16,2048]{2,1,0:T(8,128)S(1)}, f32[2,16,2048]{2,1,0:T(8,128)S(1)}, u32[]{:S(2)}, u32[]{:S(2)}) collective-permute-start(f32[2,16,2048]{2,1,0:T(8,128)S(1)} %get-tuple-element.10), channel_id=1, source_target_pairs={{0,48},{16,0},{32,16},{48,32},{1,49},{17,1},{33,17},{49,33},{2,50}... | collective-permute-start | bytes 786440 | tf_op jit(solution)/shard_map/ppermute | solution.py:19
  36.6 13.1 %collective-permute-start.11 = (f32[2,8,2048]{2,1,0:T(8,128)S(1)}, f32[2,8,2048]{2,1,0:T(8,128)S(1)}, u32[]{:S(2)}, u32[]{:S(2)}) collective-permute-start(f32[2,8,2048]{2,1,0:T(8,128)S(1)} %slice.46), channel_id=1, source_target_pairs={{0,128},{128,256},{256,384},{384,0},{1,129},{129,257},{257,385},{3... | collective-permute-start | bytes 393224 | tf_op jit(solution)/shard_map/ppermute | solution.py:19
  38.6 11.2 %collective-permute-start.12 = (f32[2,8,2048]{2,1,0:T(8,128)S(1)}, f32[2,8,2048]{2,1,0:T(8,128)S(1)}, u32[]{:S(2)}, u32[]{:S(2)}) collective-permute-start(f32[2,8,2048]{2,1,0:T(8,128)S(1)} %slice.47), channel_id=1, source_target_pairs={{0,384},{128,0},{256,128},{384,256},{1,385},{129,1},{257,129},{385... | collective-permute-start | bytes 393224 | tf_op jit(solution)/shard_map/ppermute | solution.py:19
  43.2 13.3 %collective-permute-start.3 = (f32[2,8,2048]{2,1,0:T(8,128)S(1)}, f32[2,8,2048]{2,1,0:T(8,128)S(1)}, u32[]{:S(2)}, u32[]{:S(2)}) collective-permute-start(f32[2,8,2048]{2,1,0:T(8,128)S(1)} %slice.42), channel_id=1, source_target_pairs={{0,16},{16,32},{32,48},{48,0},{1,17},{17,33},{33,49},{49,1},{2,18}... | collective-permute-start | bytes 393224 | tf_op jit(solution)/shard_map/ppermute | solution.py:19
  45.1 11.4 %collective-permute-start.4 = (f32[2,8,2048]{2,1,0:T(8,128)S(1)}, f32[2,8,2048]{2,1,0:T(8,128)S(1)}, u32[]{:S(2)}, u32[]{:S(2)}) collective-permute-start(f32[2,8,2048]{2,1,0:T(8,128)S(1)} %slice.43), channel_id=1, source_target_pairs={{0,48},{16,0},{32,16},{48,32},{1,49},{17,1},{33,17},{49,33},{2,50}... | collective-permute-start | bytes 393224 | tf_op jit(solution)/shard_map/ppermute | solution.py:19
  50.0 24.0 %collective-permute-start.14 = (f32[4,2,16,2048]{3,2,1,0:T(8,128)S(1)}, f32[4,2,16,2048]{3,2,1,0:T(8,128)S(1)}, u32[]{:S(2)}, u32[]{:S(2)}) collective-permute-start(f32[4,2,16,2048]{3,2,1,0:T(8,128)S(1)} %get-tuple-element.6), channel_id=1, source_target_pairs={{0,16},{16,32},{32,48},{48,0},{1,17},{17,33},{33,49},{49,1},{2,18}... | collective-permute-start | bytes 3145736 | tf_op jit(solution)/shard_map/ppermute | solution.py:19
  51.9 24.9 %collective-permute-start.13 = (f32[4,2,16,2048]{3,2,1,0:T(8,128)S(1)}, f32[4,2,16,2048]{3,2,1,0:T(8,128)S(1)}, u32[]{:S(2)}, u32[]{:S(2)}) collective-permute-start(f32[4,2,16,2048]{3,2,1,0:T(8,128)S(1)} %get-tuple-element.6), channel_id=1, source_target_pairs={{0,48},{16,0},{32,16},{48,32},{1,49},{17,1},{33,17},{49,33},{2,50}... | collective-permute-start | bytes 3145736 | tf_op jit(solution)/shard_map/ppermute | solution.py:19
  56.8 25.8 %collective-permute-start.6 = (f32[4,2,16,2048]{3,2,1,0:T(8,128)S(1)}, f32[4,2,16,2048]{3,2,1,0:T(8,128)}, u32[]{:S(2)}, u32[]{:S(2)}) collective-permute-start(f32[4,2,16,2048]{3,2,1,0:T(8,128)S(1)} %get-tuple-element.8), channel_id=1, source_target_pairs={{0,128},{128,256},{256,384},{384,0},{1,129},{129,257},{257,385},{3... | collective-permute-start | bytes 3145736 | tf_op jit(solution)/shard_map/ppermute | solution.py:19
  58.7 27.0 %collective-permute-start.5 = (f32[4,2,16,2048]{3,2,1,0:T(8,128)S(1)}, f32[4,2,16,2048]{3,2,1,0:T(8,128)}, u32[]{:S(2)}, u32[]{:S(2)}) collective-permute-start(f32[4,2,16,2048]{3,2,1,0:T(8,128)S(1)} %get-tuple-element.8), channel_id=1, source_target_pairs={{0,384},{128,0},{256,128},{384,256},{1,385},{129,1},{257,129},{385... | collective-permute-start | bytes 3145736 | tf_op jit(solution)/shard_map/ppermute | solution.py:19
  74.0 2.8 %copy-start = (f32[4,2,16,2048]{3,2,1,0:T(8,128)}, f32[4,2,16,2048]{3,2,1,0:T(8,128)S(1)}, u32[]{:S(2)}) copy-start(f32[4,2,16,2048]{3,2,1,0:T(8,128)S(1)} %collective-permute-done.14) | copy-start | bytes 3145732
  74.9 16.5 %collective-permute-start.15 = (f32[4,2,8,2048]{3,2,1,0:T(8,128)}, f32[4,2,8,2048]{3,2,1,0:T(8,128)}, u32[]{:S(2)}, u32[]{:S(2)}) collective-permute-start(f32[4,2,8,2048]{3,2,1,0:T(8,128)} %slice.48), channel_id=1, source_target_pairs={{0,16},{16,32},{32,48},{48,0},{1,17},{17,33},{33,49},{49,1},{2,18}... | collective-permute-start | bytes 1572872 | tf_op jit(solution)/shard_map/ppermute | solution.py:19
  76.9 1.1 copy-start.2
  78.0 13.5 %collective-permute-start.16 = (f32[4,2,8,2048]{3,2,1,0:T(8,128)}, f32[4,2,8,2048]{3,2,1,0:T(8,128)}, u32[]{:S(2)}, u32[]{:S(2)}) collective-permute-start(f32[4,2,8,2048]{3,2,1,0:T(8,128)} %slice.49), channel_id=1, source_target_pairs={{0,48},{16,0},{32,16},{48,32},{1,49},{17,1},{33,17},{49,33},{2,50}... | collective-permute-start | bytes 1572872 | tf_op jit(solution)/shard_map/ppermute | solution.py:19
  82.6 10.2 %copy-start.1 = (f32[4,2,16,2048]{3,2,1,0:T(8,128)S(1)}, f32[4,2,16,2048]{3,2,1,0:T(8,128)}, u32[]{:S(2)}) copy-start(f32[4,2,16,2048]{3,2,1,0:T(8,128)} %copy-done) | copy-start | bytes 3145732
  82.6 10.2 %copy-start.3 = (f32[4,2,16,2048]{3,2,1,0:T(8,128)S(1)}, f32[4,2,16,2048]{3,2,1,0:T(8,128)}, u32[]{:S(2)}) copy-start(f32[4,2,16,2048]{3,2,1,0:T(8,128)} %copy-done.2) | copy-start | bytes 3145732
  83.9 14.7 %collective-permute-start.7 = (f32[4,2,8,2048]{3,2,1,0:T(8,128)S(1)}, f32[4,2,8,2048]{3,2,1,0:T(8,128)S(1)}, u32[]{:S(2)}, u32[]{:S(2)}) collective-permute-start(f32[4,2,8,2048]{3,2,1,0:T(8,128)S(1)} %slice.44), channel_id=1, source_target_pairs={{0,128},{128,256},{256,384},{384,0},{1,129},{129,257},{257,385},{3... | collective-permute-start | bytes 1572872 | tf_op jit(solution)/shard_map/ppermute | solution.py:19
  86.9 11.7 %collective-permute-start.8 = (f32[4,2,8,2048]{3,2,1,0:T(8,128)S(1)}, f32[4,2,8,2048]{3,2,1,0:T(8,128)S(1)}, u32[]{:S(2)}, u32[]{:S(2)}) collective-permute-start(f32[4,2,8,2048]{3,2,1,0:T(8,128)S(1)} %slice.45), channel_id=1, source_target_pairs={{0,384},{128,0},{256,128},{384,256},{1,385},{129,1},{257,129},{385... | collective-permute-start | bytes 1572872 | tf_op jit(solution)/shard_map/ppermute | solution.py:19
  92.8 5.9 %copy-start.5 = (f32[512,2048]{1,0:T(8,128)S(1)}, f32[512,2048]{1,0:T(8,128)}, u32[]{:S(2)}) copy-start(f32[512,2048]{1,0:T(8,128)} %param.3) | copy-start | bytes 12582916
  105.2 77.5 %copy-start.4 = (f32[64,512]{1,0:T(8,128)S(1)}, f32[64,512]{1,0:T(8,128)}, u32[]{:S(2)}) copy-start(f32[64,512]{1,0:T(8,128)} %param.5) | copy-start | bytes 393220
  105.2 10.2 %collective-permute-start.17 = (f32[8,64,512]{2,1,0:T(8,128)S(1)}, f32[8,64,512]{2,1,0:T(8,128)}, u32[]{:S(2)}, u32[]{:S(2)}) collective-permute-start(f32[8,64,512]{2,1,0:T(8,128)S(1)} %dynamic-slice_bitcast_fusion), channel_id=1, source_target_pairs={{0,1},{1,0},{2,3},{3,2},{4,5},{5,4},{6,7},{7,6},{8,9},{9,8},{10,11... | collective-permute-start | bytes 3145736 | tf_op jit(solution)/shard_map/ppermute | solution.py:41
  117.0 31.4 %collective-permute-start.18 = (f32[4,64,512]{2,1,0:T(8,128)S(1)}, f32[4,64,512]{2,1,0:T(8,128)S(1)}, u32[]{:S(2)}, u32[]{:S(2)}) collective-permute-start(f32[4,64,512]{2,1,0:T(8,128)S(1)} %dynamic-slice_bitcast_fusion.1), channel_id=1, source_target_pairs={{0,2},{2,0},{4,6},{6,4},{8,10},{10,8},{12,14},{14,12},{1,3},{3,1},... | collective-permute-start | bytes 1572872 | tf_op jit(solution)/shard_map/ppermute | solution.py:41
  148.5 15.7 %collective-permute-start.19 = (f32[2,64,512]{2,1,0:T(8,128)S(1)}, f32[2,64,512]{2,1,0:T(8,128)S(1)}, u32[]{:S(2)}, u32[]{:S(2)}) collective-permute-start(f32[2,64,512]{2,1,0:T(8,128)S(1)} %dynamic-slice_bitcast_fusion.2), channel_id=1, source_target_pairs={{0,4},{2,6},{4,0},{6,2},{8,12},{10,14},{12,8},{14,10},{1,5},{3,7},... | collective-permute-start | bytes 786440 | tf_op jit(solution)/shard_map/ppermute | solution.py:41
  164.3 18.3 %collective-permute-start.20 = (f32[1,64,512]{2,1,0:T(8,128)S(1)}, f32[1,64,512]{2,1,0:T(8,128)S(1)}, u32[]{:S(2)}, u32[]{:S(2)}) collective-permute-start(f32[1,64,512]{2,1,0:T(8,128)S(1)} %constant_dynamic-slice_fusion), channel_id=1, source_target_pairs={{0,8},{2,10},{4,12},{6,14},{8,0},{10,2},{12,4},{14,6},{1,9},{3,11}... | collective-permute-start | bytes 393224 | tf_op jit(solution)/shard_map/ppermute | solution.py:41

commit v5 on v4

--- a/solution.py
+++ b/solution.py
@@ -65,15 +65,13 @@
     rows = green.shape[0]
     partner = swap(green, "zh", 1)
     first = lax.axis_index("zh") == 0
-    g = jnp.stack([jnp.where(first, green, partner), jnp.where(first, partner, green)])
-    h = rows // 2
 
     def mm(t):
         return contract(t.reshape(-1, t.shape[-1]), rotated).reshape(t.shape[:-1] + (rotated.shape[0],))
 
-    v1 = ring(ring(g[:, :h], "x"), "y")
-    v2 = ring(ring(g[:, h:], "y"), "x")
-    o = jnp.concatenate([mm(v1), mm(v2).transpose(1, 0, 2, 3, 4)], axis=3)
+    own = mm(ring(ring(green, "x"), "y"))
+    other = mm(ring(ring(partner, "y"), "x")).transpose(1, 0, 2, 3)
+    o = jnp.roll(jnp.stack([own, other], axis=2), lax.axis_index("zh"), axis=2)
     o = jnp.roll(o, lax.axis_index("y"), axis=0)
     o = jnp.roll(o, lax.axis_index("x"), axis=1)
     part = o.transpose(0, 2, 1, 3, 4)

time: 184 us -> 183 us (level)
  waiting for transfers between devices: 55.2 us -> 48.6 us
  starting transfers between devices: 106 us -> 110 us
    ppermute x5, waiting for transfers between devices: 44.4 us -> 38.8 us  [swap(): return lax.ppermute(v, axis, [(i, i ^ bit) for i in range(n)])]
    ppermute x5, starting transfers between devices: 53 us -> 55.9 us  [swap(): return lax.ppermute(v, axis, [(i, i ^ bit) for i in range(n)])]
  transfers between devices with their start and end apart: 21 -> 21, of which waited for: 6 -> 6; matrix products, arithmetic and copies ran while one was open for 6% -> 7% of each run, Pallas kernels for 0% -> 0%
where the time goes in v5:
time: 183 us; the launch traced here: 182 us
  starting transfers between devices  110 us (60%)
  waiting for transfers between devices  48.6 us (27%)
  matrix products  11 us (6%)
  other arithmetic  6.7 us (4%)
  local copies, waits for them, and re-layouts  4.71 us (3%)
    ppermute x5, starting transfers between devices, swap(): return lax.ppermute(v, axis, [(i, i ^ bit) for i in range(n)])  55.9 us
    ppermute x16, starting transfers between devices, shift(): return lax.ppermute(v, axis, [(i, (i + k) % n) for i in range(n)])  53.9 us
    ppermute x5, waiting for transfers between devices, swap(): return lax.ppermute(v, axis, [(i, i ^ bit) for i in range(n)])  38.8 us
    dot_general x2, matrix products, contract(): lax.dot_general(rows, rotated, (((1,), (1,)), ((), ())), precision=lax.Pr...  11 us
    ppermute x16, waiting for transfers between devices, shift(): return lax.ppermute(v, axis, [(i, (i + k) % n) for i in range(n)])  9.85 us
  transfers between devices with their start and end apart: 21, of which 6 were waited for; matrix products, arithmetic and copies ran while one was open for 7% of the time, Pallas kernels for 0%

profile of v5, /device:TPU:1, one launch (start us, length us, event | category | flops | bytes accessed | tf_op | source)
XLA Modules:
  0.0 181.6 jit_solution(5220893997765121942)
XLA Ops:
  0.0 3.9 %collective-permute-start.1 = (f32[32,2048]{1,0:T(8,128)}, f32[32,2048]{1,0:T(8,128)S(1)}, u32[]{:S(2)}, u32[]{:S(2)}) collective-permute-start(f32[32,2048]{1,0:T(8,128)} %param.4), channel_id=1, source_target_pairs={{0,16},{16,32},{32,48},{48,0},{1,17},{17,33},{33,49},{49,1},{2,18}... | collective-permute-start | bytes 786440 | tf_op jit(solution)/shard_map/ppermute | solution.py:19
  3.9 3.2 %collective-permute-start = (f32[32,2048]{1,0:T(8,128)}, f32[32,2048]{1,0:T(8,128)S(1)}, u32[]{:S(2)}, u32[]{:S(2)}) collective-permute-start(f32[32,2048]{1,0:T(8,128)} %param.4), channel_id=1, source_target_pairs={{0,48},{16,0},{32,16},{48,32},{1,49},{17,1},{33,17},{49,33},{2,50}... | collective-permute-start | bytes 786440 | tf_op jit(solution)/shard_map/ppermute | solution.py:19
  7.1 15.6 %collective-permute-start.8 = (f32[32,2048]{1,0:T(8,128)}, f32[32,2048]{1,0:T(8,128)S(1)}, u32[]{:S(2)}, u32[]{:S(2)}) collective-permute-start(f32[32,2048]{1,0:T(8,128)} %param.4), channel_id=1, source_target_pairs={{0,64},{64,0},{1,65},{65,1},{2,66},{66,2},{3,67},{67,3},{4,68},{68... | collective-permute-start | bytes 786440 | tf_op jit(solution)/shard_map/ppermute | solution.py:41
  22.8 1.9 %collective-permute-start.2 = (f32[16,2048]{1,0:T(8,128)S(1)}, f32[16,2048]{1,0:T(8,128)S(1)}, u32[]{:S(2)}, u32[]{:S(2)}) collective-permute-start(f32[16,2048]{1,0:T(8,128)S(1)} %slice.32), channel_id=1, source_target_pairs={{0,16},{16,32},{32,48},{48,0},{1,17},{17,33},{33,49},{49,1},{2,18}... | collective-permute-start | bytes 393224 | tf_op jit(solution)/shard_map/ppermute | solution.py:19
  24.8 4.6 %collective-permute-start.3 = (f32[16,2048]{1,0:T(8,128)S(1)}, f32[16,2048]{1,0:T(8,128)S(1)}, u32[]{:S(2)}, u32[]{:S(2)}) collective-permute-start(f32[16,2048]{1,0:T(8,128)S(1)} %slice.33), channel_id=1, source_target_pairs={{0,48},{16,0},{32,16},{48,32},{1,49},{17,1},{33,17},{49,33},{2,50}... | collective-permute-start | bytes 393224 | tf_op jit(solution)/shard_map/ppermute | solution.py:19
  29.3 3.2 %collective-permute-start.10 = (f32[32,2048]{1,0:T(8,128)S(1)}, f32[32,2048]{1,0:T(8,128)S(1)}, u32[]{:S(2)}, u32[]{:S(2)}) collective-permute-start(f32[32,2048]{1,0:T(8,128)S(1)} %collective-permute-done.8), channel_id=1, source_target_pairs={{0,128},{128,256},{256,384},{384,0},{1,129},{129,257},{257,385},{3... | collective-permute-start | bytes 786440 | tf_op jit(solution)/shard_map/ppermute | solution.py:19
  32.6 3.4 %collective-permute-start.9 = (f32[32,2048]{1,0:T(8,128)S(1)}, f32[32,2048]{1,0:T(8,128)S(1)}, u32[]{:S(2)}, u32[]{:S(2)}) collective-permute-start(f32[32,2048]{1,0:T(8,128)S(1)} %collective-permute-done.8), channel_id=1, source_target_pairs={{0,384},{128,0},{256,128},{384,256},{1,385},{129,1},{257,129},{385... | collective-permute-start | bytes 786440 | tf_op jit(solution)/shard_map/ppermute | solution.py:19
  36.0 1.8 collective-permute-done.10
  37.8 1.9 %collective-permute-start.11 = (f32[16,2048]{1,0:T(8,128)S(1)}, f32[16,2048]{1,0:T(8,128)S(1)}, u32[]{:S(2)}, u32[]{:S(2)}) collective-permute-start(f32[16,2048]{1,0:T(8,128)S(1)} %slice.36), channel_id=1, source_target_pairs={{0,128},{128,256},{256,384},{384,0},{1,129},{129,257},{257,385},{3... | collective-permute-start | bytes 393224 | tf_op jit(solution)/shard_map/ppermute | solution.py:19
  39.7 4.6 %collective-permute-start.12 = (f32[16,2048]{1,0:T(8,128)S(1)}, f32[16,2048]{1,0:T(8,128)S(1)}, u32[]{:S(2)}, u32[]{:S(2)}) collective-permute-start(f32[16,2048]{1,0:T(8,128)S(1)} %slice.37), channel_id=1, source_target_pairs={{0,384},{128,0},{256,128},{384,256},{1,385},{129,1},{257,129},{385... | collective-permute-start | bytes 393224 | tf_op jit(solution)/shard_map/ppermute | solution.py:19
  44.3 1.2 fusion.37
  45.5 1.9 %collective-permute-start.5 = (f32[4,32,2048]{2,1,0:T(8,128)S(1)}, f32[4,32,2048]{2,1,0:T(8,128)S(1)}, u32[]{:S(2)}, u32[]{:S(2)}) collective-permute-start(f32[4,32,2048]{2,1,0:T(8,128)S(1)} %get-tuple-element.8), channel_id=1, source_target_pairs={{0,128},{128,256},{256,384},{384,0},{1,129},{129,257},{257,385},{3... | collective-permute-start | bytes 3145736 | tf_op jit(solution)/shard_map/ppermute | solution.py:19
  47.4 4.6 %collective-permute-start.4 = (f32[4,32,2048]{2,1,0:T(8,128)S(1)}, f32[4,32,2048]{2,1,0:T(8,128)S(1)}, u32[]{:S(2)}, u32[]{:S(2)}) collective-permute-start(f32[4,32,2048]{2,1,0:T(8,128)S(1)} %get-tuple-element.8), channel_id=1, source_target_pairs={{0,384},{128,0},{256,128},{384,256},{1,385},{129,1},{257,129},{385... | collective-permute-start | bytes 3145736 | tf_op jit(solution)/shard_map/ppermute | solution.py:19
  52.1 0.2 fusion.36
  52.3 1.9 %collective-permute-start.14 = (f32[4,32,2048]{2,1,0:T(8,128)S(1)}, f32[4,32,2048]{2,1,0:T(8,128)}, u32[]{:S(2)}, u32[]{:S(2)}) collective-permute-start(f32[4,32,2048]{2,1,0:T(8,128)S(1)} %get-tuple-element.6), channel_id=1, source_target_pairs={{0,16},{16,32},{32,48},{48,0},{1,17},{17,33},{33,49},{49,1},{2,18}... | collective-permute-start | bytes 3145736 | tf_op jit(solution)/shard_map/ppermute | solution.py:19
  54.2 4.6 %collective-permute-start.13 = (f32[4,32,2048]{2,1,0:T(8,128)S(1)}, f32[4,32,2048]{2,1,0:T(8,128)}, u32[]{:S(2)}, u32[]{:S(2)}) collective-permute-start(f32[4,32,2048]{2,1,0:T(8,128)S(1)} %get-tuple-element.6), channel_id=1, source_target_pairs={{0,48},{16,0},{32,16},{48,32},{1,49},{17,1},{33,17},{49,33},{2,50}... | collective-permute-start | bytes 3145736 | tf_op jit(solution)/shard_map/ppermute | solution.py:19
  58.8 8.0 %collective-permute-done.5 = f32[4,32,2048]{2,1,0:T(8,128)S(1)} collective-permute-done((f32[4,32,2048]{2,1,0:T(8,128)S(1)}, f32[4,32,2048]{2,1,0:T(8,128)S(1)}, u32[]{:S(2)}, u32[]{:S(2)}) %collective-permute-start.5) | collective-permute-done | bytes 1048608 | tf_op jit(solution)/shard_map/ppermute | solution.py:19
  66.9 0.9 slice.34
  67.7 1.9 %collective-permute-start.6 = (f32[4,16,2048]{2,1,0:T(8,128)}, f32[4,16,2048]{2,1,0:T(8,128)}, u32[]{:S(2)}, u32[]{:S(2)}) collective-permute-start(f32[4,16,2048]{2,1,0:T(8,128)} %slice.34), channel_id=1, source_target_pairs={{0,128},{128,256},{256,384},{384,0},{1,129},{129,257},{257,385},{3... | collective-permute-start | bytes 1572872 | tf_op jit(solution)/shard_map/ppermute | solution.py:19
  69.7 0.9 slice.35
  70.6 0.2 copy-done.2
  70.8 4.6 %collective-permute-start.7 = (f32[4,16,2048]{2,1,0:T(8,128)}, f32[4,16,2048]{2,1,0:T(8,128)}, u32[]{:S(2)}, u32[]{:S(2)}) collective-permute-start(f32[4,16,2048]{2,1,0:T(8,128)} %slice.35), channel_id=1, source_target_pairs={{0,384},{128,0},{256,128},{384,256},{1,385},{129,1},{257,129},{385... | collective-permute-start | bytes 1572872 | tf_op jit(solution)/shard_map/ppermute | solution.py:19
  75.5 1.2 slice.38
  76.7 4.6 %collective-permute-start.15 = (f32[4,16,2048]{2,1,0:T(8,128)S(1)}, f32[4,16,2048]{2,1,0:T(8,128)S(1)}, u32[]{:S(2)}, u32[]{:S(2)}) collective-permute-start(f32[4,16,2048]{2,1,0:T(8,128)S(1)} %slice.38), channel_id=1, source_target_pairs={{0,16},{16,32},{32,48},{48,0},{1,17},{17,33},{33,49},{49,1},{2,18}... | collective-permute-start | bytes 1572872 | tf_op jit(solution)/shard_map/ppermute | solution.py:19
  81.3 1.1 slice.39
  82.4 3.2 %collective-permute-start.16 = (f32[4,16,2048]{2,1,0:T(8,128)S(1)}, f32[4,16,2048]{2,1,0:T(8,128)S(1)}, u32[]{:S(2)}, u32[]{:S(2)}) collective-permute-start(f32[4,16,2048]{2,1,0:T(8,128)S(1)} %slice.39), channel_id=1, source_target_pairs={{0,48},{16,0},{32,16},{48,32},{1,49},{17,1},{33,17},{49,33},{2,50}... | collective-permute-start | bytes 1572872 | tf_op jit(solution)/shard_map/ppermute | solution.py:19
  85.6 1.3 maximum_bitcast_fusion
  86.9 0.0 copy-start.5
  86.9 6.0 %fusion.29 = f32[4,4,1,32,512]{4,3,1,0,2:T(8,128)S(1)} fusion(f32[512,2048]{1,0:T(8,128)} %param.3, f32[1,4,32,2048]{3,2,1,0:T(8,128)S(1)} %bitcast.76, f32[1,4,32,2048]{3,2,1,0:T(8,128)S(1)} %maximum_bitcast_fusion, f32[1,4,32,2048]{3,2,1,0:T(8,128)S(1)} %bitcast.77, f32[1,4,32,2048]{3,2,1,0:T(8,128)S(1)} %get-tuple-element.7), kind=kOutput, calls=%fused_computation.33 | convolution fusion | flops 3224371200 | bytes 9437184 | tf_op jit(solution)/shard_map/dot_general | solution.py:13
  93.0 0.1 maximum_bitcast_fusion.1
  93.1 5.0 %fusion.24 = f32[4,4,1,32,512]{4,3,1,0,2:T(8,128)S(1)} fusion(f32[512,2048]{1,0:T(8,128)S(1)} %copy-done.5, f32[1,4,32,2048]{3,2,0,1:T(8,128)} %bitcast.21, f32[1,4,32,2048]{3,2,0,1:T(8,128)S(1)} %maximum_bitcast_fusion.1, f32[1,4,32,2048]{3,2,0,1:T(8,128)} %bitcast.18, f32[1,4,32,2048]{3,2,0,1:T(8,128)S(1)} %get-tuple-element.5), kind=kOutput, calls=%fused_computation.32 | convolution fusion | flops 3224371200 | bytes 9437184 | tf_op jit(solution)/shard_map/dot_general | solution.py:13
  98.1 0.5 fusion.23
  98.7 0.5 fusion.20
  99.2 0.5 fusion.19
  99.8 0.2 copy.10
  99.9 0.1 dynamic-slice_bitcast_fusion
  100.0 0.0 copy-start.4
  100.0 12.0 %collective-permute-start.17 = (f32[8,64,512]{2,1,0:T(8,128)S(1)}, f32[8,64,512]{2,1,0:T(8,128)}, u32[]{:S(2)}, u32[]{:S(2)}) collective-permute-start(f32[8,64,512]{2,1,0:T(8,128)S(1)} %dynamic-slice_bitcast_fusion), channel_id=1, source_target_pairs={{0,1},{1,0},{2,3},{3,2},{4,5},{5,4},{6,7},{7,6},{8,9},{9,8},{10,11... | collective-permute-start | bytes 3145736 | tf_op jit(solution)/shard_map/ppermute | solution.py:41
  112.1 2.4 %collective-permute-done.17 = f32[8,64,512]{2,1,0:T(8,128)} collective-permute-done((f32[8,64,512]{2,1,0:T(8,128)S(1)}, f32[8,64,512]{2,1,0:T(8,128)}, u32[]{:S(2)}, u32[]{:S(2)}) %collective-permute-start.17) | collective-permute-done | bytes 1048608 | tf_op jit(solution)/shard_map/ppermute | solution.py:41
  114.5 1.4 bitcast_add_fusion
  116.0 17.2 %collective-permute-start.18 = (f32[4,64,512]{2,1,0:T(8,128)S(1)}, f32[4,64,512]{2,1,0:T(8,128)S(1)}, u32[]{:S(2)}, u32[]{:S(2)}) collective-permute-start(f32[4,64,512]{2,1,0:T(8,128)S(1)} %dynamic-slice_bitcast_fusion.1), channel_id=1, source_target_pairs={{0,2},{2,0},{4,6},{6,4},{8,10},{10,8},{12,14},{14,12},{1,3},{3,1},... | collective-permute-start | bytes 1572872 | tf_op jit(solution)/shard_map/ppermute | solution.py:41
  133.3 11.9 %collective-permute-done.18 = f32[4,64,512]{2,1,0:T(8,128)S(1)} collective-permute-done((f32[4,64,512]{2,1,0:T(8,128)S(1)}, f32[4,64,512]{2,1,0:T(8,128)S(1)}, u32[]{:S(2)}, u32[]{:S(2)}) %collective-permute-start.18) | collective-permute-done | bytes 524320 | tf_op jit(solution)/shard_map/ppermute | solution.py:41
  145.1 0.1 bitcast_add_fusion.1
  145.3 1.9 %collective-permute-start.19 = (f32[2,64,512]{2,1,0:T(8,128)S(1)}, f32[2,64,512]{2,1,0:T(8,128)S(1)}, u32[]{:S(2)}, u32[]{:S(2)}) collective-permute-start(f32[2,64,512]{2,1,0:T(8,128)S(1)} %dynamic-slice_bitcast_fusion.2), channel_id=1, source_target_pairs={{0,4},{2,6},{4,0},{6,2},{8,12},{10,14},{12,8},{14,10},{1,5},{3,7},... | collective-permute-start | bytes 786440 | tf_op jit(solution)/shard_map/ppermute | solution.py:41
  147.2 13.8 %collective-permute-done.19 = f32[2,64,512]{2,1,0:T(8,128)S(1)} collective-permute-done((f32[2,64,512]{2,1,0:T(8,128)S(1)}, f32[2,64,512]{2,1,0:T(8,128)S(1)}, u32[]{:S(2)}, u32[]{:S(2)}) %collective-permute-start.19) | collective-permute-done | bytes 262176 | tf_op jit(solution)/shard_map/ppermute | solution.py:41
  161.1 9.0 %collective-permute-start.20 = (f32[1,64,512]{2,1,0:T(8,128)S(1)}, f32[1,64,512]{2,1,0:T(8,128)S(1)}, u32[]{:S(2)}, u32[]{:S(2)}) collective-permute-start(f32[1,64,512]{2,1,0:T(8,128)S(1)} %constant_dynamic-slice_fusion), channel_id=1, source_target_pairs={{0,8},{2,10},{4,12},{6,14},{8,0},{10,2},{12,4},{14,6},{1,9},{3,11}... | collective-permute-start | bytes 393224 | tf_op jit(solution)/shard_map/ppermute | solution.py:41
  170.1 10.8 %collective-permute-done.20 = f32[1,64,512]{2,1,0:T(8,128)S(1)} collective-permute-done((f32[1,64,512]{2,1,0:T(8,128)S(1)}, f32[1,64,512]{2,1,0:T(8,128)S(1)}, u32[]{:S(2)}, u32[]{:S(2)}) %collective-permute-start.20) | collective-permute-done | bytes 131104 | tf_op jit(solution)/shard_map/ppermute | solution.py:41
  180.9 0.7 bitcast_subtract_fusion
  (34 shorter events, 0.3 us)
Async XLA Ops:
  0.0 22.8 %collective-permute-start.1 = (f32[32,2048]{1,0:T(8,128)}, f32[32,2048]{1,0:T(8,128)S(1)}, u32[]{:S(2)}, u32[]{:S(2)}) collective-permute-start(f32[32,2048]{1,0:T(8,128)} %param.4), channel_id=1, source_target_pairs={{0,16},{16,32},{32,48},{48,0},{1,17},{17,33},{33,49},{49,1},{2,18}... | collective-permute-start | bytes 786440 | tf_op jit(solution)/shard_map/ppermute | solution.py:19
  3.9 20.8 %collective-permute-start = (f32[32,2048]{1,0:T(8,128)}, f32[32,2048]{1,0:T(8,128)S(1)}, u32[]{:S(2)}, u32[]{:S(2)}) collective-permute-start(f32[32,2048]{1,0:T(8,128)} %param.4), channel_id=1, source_target_pairs={{0,48},{16,0},{32,16},{48,32},{1,49},{17,1},{33,17},{49,33},{2,50}... | collective-permute-start | bytes 786440 | tf_op jit(solution)/shard_map/ppermute | solution.py:19
  7.1 22.2 %collective-permute-start.8 = (f32[32,2048]{1,0:T(8,128)}, f32[32,2048]{1,0:T(8,128)S(1)}, u32[]{:S(2)}, u32[]{:S(2)}) collective-permute-start(f32[32,2048]{1,0:T(8,128)} %param.4), channel_id=1, source_target_pairs={{0,64},{64,0},{1,65},{65,1},{2,66},{66,2},{3,67},{67,3},{4,68},{68... | collective-permute-start | bytes 786440 | tf_op jit(solution)/shard_map/ppermute | solution.py:41
  22.8 13.1 %collective-permute-start.2 = (f32[16,2048]{1,0:T(8,128)S(1)}, f32[16,2048]{1,0:T(8,128)S(1)}, u32[]{:S(2)}, u32[]{:S(2)}) collective-permute-start(f32[16,2048]{1,0:T(8,128)S(1)} %slice.32), channel_id=1, source_target_pairs={{0,16},{16,32},{32,48},{48,0},{1,17},{17,33},{33,49},{49,1},{2,18}... | collective-permute-start | bytes 393224 | tf_op jit(solution)/shard_map/ppermute | solution.py:19
  24.8 11.2 %collective-permute-start.3 = (f32[16,2048]{1,0:T(8,128)S(1)}, f32[16,2048]{1,0:T(8,128)S(1)}, u32[]{:S(2)}, u32[]{:S(2)}) collective-permute-start(f32[16,2048]{1,0:T(8,128)S(1)} %slice.33), channel_id=1, source_target_pairs={{0,48},{16,0},{32,16},{48,32},{1,49},{17,1},{33,17},{49,33},{2,50}... | collective-permute-start | bytes 393224 | tf_op jit(solution)/shard_map/ppermute | solution.py:19
  29.3 8.4 %collective-permute-start.10 = (f32[32,2048]{1,0:T(8,128)S(1)}, f32[32,2048]{1,0:T(8,128)S(1)}, u32[]{:S(2)}, u32[]{:S(2)}) collective-permute-start(f32[32,2048]{1,0:T(8,128)S(1)} %collective-permute-done.8), channel_id=1, source_target_pairs={{0,128},{128,256},{256,384},{384,0},{1,129},{129,257},{257,385},{3... | collective-permute-start | bytes 786440 | tf_op jit(solution)/shard_map/ppermute | solution.py:19
  32.6 7.1 %collective-permute-start.9 = (f32[32,2048]{1,0:T(8,128)S(1)}, f32[32,2048]{1,0:T(8,128)S(1)}, u32[]{:S(2)}, u32[]{:S(2)}) collective-permute-start(f32[32,2048]{1,0:T(8,128)S(1)} %collective-permute-done.8), channel_id=1, source_target_pairs={{0,384},{128,0},{256,128},{384,256},{1,385},{129,1},{257,129},{385... | collective-permute-start | bytes 786440 | tf_op jit(solution)/shard_map/ppermute | solution.py:19
  37.8 14.2 %collective-permute-start.11 = (f32[16,2048]{1,0:T(8,128)S(1)}, f32[16,2048]{1,0:T(8,128)S(1)}, u32[]{:S(2)}, u32[]{:S(2)}) collective-permute-start(f32[16,2048]{1,0:T(8,128)S(1)} %slice.36), channel_id=1, source_target_pairs={{0,128},{128,256},{256,384},{384,0},{1,129},{129,257},{257,385},{3... | collective-permute-start | bytes 393224 | tf_op jit(solution)/shard_map/ppermute | solution.py:19
  39.7 12.3 %collective-permute-start.12 = (f32[16,2048]{1,0:T(8,128)S(1)}, f32[16,2048]{1,0:T(8,128)S(1)}, u32[]{:S(2)}, u32[]{:S(2)}) collective-permute-start(f32[16,2048]{1,0:T(8,128)S(1)} %slice.37), channel_id=1, source_target_pairs={{0,384},{128,0},{256,128},{384,256},{1,385},{129,1},{257,129},{385... | collective-permute-start | bytes 393224 | tf_op jit(solution)/shard_map/ppermute | solution.py:19
  45.5 21.3 %collective-permute-start.5 = (f32[4,32,2048]{2,1,0:T(8,128)S(1)}, f32[4,32,2048]{2,1,0:T(8,128)S(1)}, u32[]{:S(2)}, u32[]{:S(2)}) collective-permute-start(f32[4,32,2048]{2,1,0:T(8,128)S(1)} %get-tuple-element.8), channel_id=1, source_target_pairs={{0,128},{128,256},{256,384},{384,0},{1,129},{129,257},{257,385},{3... | collective-permute-start | bytes 3145736 | tf_op jit(solution)/shard_map/ppermute | solution.py:19
  47.4 22.2 %collective-permute-start.4 = (f32[4,32,2048]{2,1,0:T(8,128)S(1)}, f32[4,32,2048]{2,1,0:T(8,128)S(1)}, u32[]{:S(2)}, u32[]{:S(2)}) collective-permute-start(f32[4,32,2048]{2,1,0:T(8,128)S(1)} %get-tuple-element.8), channel_id=1, source_target_pairs={{0,384},{128,0},{256,128},{384,256},{1,385},{129,1},{257,129},{385... | collective-permute-start | bytes 3145736 | tf_op jit(solution)/shard_map/ppermute | solution.py:19
  52.3 23.1 %collective-permute-start.14 = (f32[4,32,2048]{2,1,0:T(8,128)S(1)}, f32[4,32,2048]{2,1,0:T(8,128)}, u32[]{:S(2)}, u32[]{:S(2)}) collective-permute-start(f32[4,32,2048]{2,1,0:T(8,128)S(1)} %get-tuple-element.6), channel_id=1, source_target_pairs={{0,16},{16,32},{32,48},{48,0},{1,17},{17,33},{33,49},{49,1},{2,18}... | collective-permute-start | bytes 3145736 | tf_op jit(solution)/shard_map/ppermute | solution.py:19
  54.2 27.1 %collective-permute-start.13 = (f32[4,32,2048]{2,1,0:T(8,128)S(1)}, f32[4,32,2048]{2,1,0:T(8,128)}, u32[]{:S(2)}, u32[]{:S(2)}) collective-permute-start(f32[4,32,2048]{2,1,0:T(8,128)S(1)} %get-tuple-element.6), channel_id=1, source_target_pairs={{0,48},{16,0},{32,16},{48,32},{1,49},{17,1},{33,17},{49,33},{2,50}... | collective-permute-start | bytes 3145736 | tf_op jit(solution)/shard_map/ppermute | solution.py:19
  66.8 2.8 %copy-start = (f32[4,32,2048]{2,1,0:T(8,128)}, f32[4,32,2048]{2,1,0:T(8,128)S(1)}, u32[]{:S(2)}) copy-start(f32[4,32,2048]{2,1,0:T(8,128)S(1)} %collective-permute-done.5) | copy-start | bytes 3145732
  67.7 17.9 %collective-permute-start.6 = (f32[4,16,2048]{2,1,0:T(8,128)}, f32[4,16,2048]{2,1,0:T(8,128)}, u32[]{:S(2)}, u32[]{:S(2)}) collective-permute-start(f32[4,16,2048]{2,1,0:T(8,128)} %slice.34), channel_id=1, source_target_pairs={{0,128},{128,256},{256,384},{384,0},{1,129},{129,257},{257,385},{3... | collective-permute-start | bytes 1572872 | tf_op jit(solution)/shard_map/ppermute | solution.py:19
  69.7 1.1 copy-start.2
  70.8 14.8 %collective-permute-start.7 = (f32[4,16,2048]{2,1,0:T(8,128)}, f32[4,16,2048]{2,1,0:T(8,128)}, u32[]{:S(2)}, u32[]{:S(2)}) collective-permute-start(f32[4,16,2048]{2,1,0:T(8,128)} %slice.35), channel_id=1, source_target_pairs={{0,384},{128,0},{256,128},{384,256},{1,385},{129,1},{257,129},{385... | collective-permute-start | bytes 1572872 | tf_op jit(solution)/shard_map/ppermute | solution.py:19
  75.4 11.5 %copy-start.1 = (f32[4,32,2048]{2,1,0:T(8,128)S(1)}, f32[4,32,2048]{2,1,0:T(8,128)}, u32[]{:S(2)}) copy-start(f32[4,32,2048]{2,1,0:T(8,128)} %copy-done) | copy-start | bytes 3145732
  75.4 11.5 %copy-start.3 = (f32[4,32,2048]{2,1,0:T(8,128)S(1)}, f32[4,32,2048]{2,1,0:T(8,128)}, u32[]{:S(2)}) copy-start(f32[4,32,2048]{2,1,0:T(8,128)} %copy-done.2) | copy-start | bytes 3145732
  76.7 16.3 %collective-permute-start.15 = (f32[4,16,2048]{2,1,0:T(8,128)S(1)}, f32[4,16,2048]{2,1,0:T(8,128)S(1)}, u32[]{:S(2)}, u32[]{:S(2)}) collective-permute-start(f32[4,16,2048]{2,1,0:T(8,128)S(1)} %slice.38), channel_id=1, source_target_pairs={{0,16},{16,32},{32,48},{48,0},{1,17},{17,33},{33,49},{49,1},{2,18}... | collective-permute-start | bytes 1572872 | tf_op jit(solution)/shard_map/ppermute | solution.py:19
  82.4 10.6 %collective-permute-start.16 = (f32[4,16,2048]{2,1,0:T(8,128)S(1)}, f32[4,16,2048]{2,1,0:T(8,128)S(1)}, u32[]{:S(2)}, u32[]{:S(2)}) collective-permute-start(f32[4,16,2048]{2,1,0:T(8,128)S(1)} %slice.39), channel_id=1, source_target_pairs={{0,48},{16,0},{32,16},{48,32},{1,49},{17,1},{33,17},{49,33},{2,50}... | collective-permute-start | bytes 1572872 | tf_op jit(solution)/shard_map/ppermute | solution.py:19
  86.9 6.2 %copy-start.5 = (f32[512,2048]{1,0:T(8,128)S(1)}, f32[512,2048]{1,0:T(8,128)}, u32[]{:S(2)}) copy-start(f32[512,2048]{1,0:T(8,128)} %param.3) | copy-start | bytes 12582916
  100.0 80.8 %copy-start.4 = (f32[64,512]{1,0:T(8,128)S(1)}, f32[64,512]{1,0:T(8,128)}, u32[]{:S(2)}) copy-start(f32[64,512]{1,0:T(8,128)} %param.5) | copy-start | bytes 393220
  100.0 14.4 %collective-permute-start.17 = (f32[8,64,512]{2,1,0:T(8,128)S(1)}, f32[8,64,512]{2,1,0:T(8,128)}, u32[]{:S(2)}, u32[]{:S(2)}) collective-permute-start(f32[8,64,512]{2,1,0:T(8,128)S(1)} %dynamic-slice_bitcast_fusion), channel_id=1, source_target_pairs={{0,1},{1,0},{2,3},{3,2},{4,5},{5,4},{6,7},{7,6},{8,9},{9,8},{10,11... | collective-permute-start | bytes 3145736 | tf_op jit(solution)/shard_map/ppermute | solution.py:41
  116.0 29.2 %collective-permute-start.18 = (f32[4,64,512]{2,1,0:T(8,128)S(1)}, f32[4,64,512]{2,1,0:T(8,128)S(1)}, u32[]{:S(2)}, u32[]{:S(2)}) collective-permute-start(f32[4,64,512]{2,1,0:T(8,128)S(1)} %dynamic-slice_bitcast_fusion.1), channel_id=1, source_target_pairs={{0,2},{2,0},{4,6},{6,4},{8,10},{10,8},{12,14},{14,12},{1,3},{3,1},... | collective-permute-start | bytes 1572872 | tf_op jit(solution)/shard_map/ppermute | solution.py:41
  145.3 15.7 %collective-permute-start.19 = (f32[2,64,512]{2,1,0:T(8,128)S(1)}, f32[2,64,512]{2,1,0:T(8,128)S(1)}, u32[]{:S(2)}, u32[]{:S(2)}) collective-permute-start(f32[2,64,512]{2,1,0:T(8,128)S(1)} %dynamic-slice_bitcast_fusion.2), channel_id=1, source_target_pairs={{0,4},{2,6},{4,0},{6,2},{8,12},{10,14},{12,8},{14,10},{1,5},{3,7},... | collective-permute-start | bytes 786440 | tf_op jit(solution)/shard_map/ppermute | solution.py:41
  161.1 19.8 %collective-permute-start.20 = (f32[1,64,512]{2,1,0:T(8,128)S(1)}, f32[1,64,512]{2,1,0:T(8,128)S(1)}, u32[]{:S(2)}, u32[]{:S(2)}) collective-permute-start(f32[1,64,512]{2,1,0:T(8,128)S(1)} %constant_dynamic-slice_fusion), channel_id=1, source_target_pairs={{0,8},{2,10},{4,12},{6,14},{8,0},{10,2},{12,4},{14,6},{1,9},{3,11}... | collective-permute-start | bytes 393224 | tf_op jit(solution)/shard_map/ppermute | solution.py:41

commit v6 on v5

--- a/solution.py
+++ b/solution.py
@@ -19,7 +19,7 @@
     return lax.ppermute(v, axis, [(i, (i + k) % n) for i in range(n)])
 
 
-def ring(v, axis):
+def ring(v, axis, split=True):
     n = lax.axis_size(axis)
     got = {0: v}
     f = b = v
@@ -28,7 +28,9 @@
         got[n - s] = f
         b = shift(b, axis, -1)
         got[s] = b
-    if n % 2 == 0:
+    if n % 2 == 0 and not split:
+        got[n // 2] = shift(f, axis, 1)
+    elif n % 2 == 0:
         h = v.shape[-2] // 2
         lo = shift(f[..., :h, :], axis, 1)
         hi = shift(b[..., h:, :], axis, -1)
@@ -69,8 +71,8 @@
     def mm(t):
         return contract(t.reshape(-1, t.shape[-1]), rotated).reshape(t.shape[:-1] + (rotated.shape[0],))
 
-    own = mm(ring(ring(green, "x"), "y"))
-    other = mm(ring(ring(partner, "y"), "x")).transpose(1, 0, 2, 3)
+    own = mm(ring(ring(green, "x", split=False), "y"))
+    other = mm(ring(ring(partner, "y", split=False), "x")).transpose(1, 0, 2, 3)
     o = jnp.roll(jnp.stack([own, other], axis=2), lax.axis_index("zh"), axis=2)
     o = jnp.roll(o, lax.axis_index("y"), axis=0)
     o = jnp.roll(o, lax.axis_index("x"), axis=1)

time: 183 us -> 191 us (1.044)
  waiting for transfers between devices: 48.6 us -> 72.6 us
  starting transfers between devices: 110 us -> 94.7 us
    ppermute x16 -> x14, waiting for transfers between devices: 9.85 us -> 33.8 us  [shift(): return lax.ppermute(v, axis, [(i, (i + k) % n) for i in range(n)])]
    ppermute x16 -> x14, starting transfers between devices: 53.9 us -> 44.4 us  [shift(): return lax.ppermute(v, axis, [(i, (i + k) % n) for i in range(n)])]
    ppermute x5, starting transfers between devices: 55.9 us -> 50.3 us  [swap(): return lax.ppermute(v, axis, [(i, i ^ bit) for i in range(n)])]
  transfers between devices with their start and end apart: 21 -> 19, of which waited for: 6 -> 7; matrix products, arithmetic and copies ran while one was open for 7% -> 7% of each run, Pallas kernels for 0% -> 0%
where the time goes in v6:
time: 191 us; the launch traced here: 190 us
  starting transfers between devices  94.7 us (50%)
  waiting for transfers between devices  72.6 us (38%)
  matrix products  11 us (6%)
  other arithmetic  6.66 us (3%)
  local copies, waits for them, and re-layouts  4.54 us (2%)
    ppermute x5, starting transfers between devices, swap(): return lax.ppermute(v, axis, [(i, i ^ bit) for i in range(n)])  50.3 us
    ppermute x14, starting transfers between devices, shift(): return lax.ppermute(v, axis, [(i, (i + k) % n) for i in range(n)])  44.4 us
    ppermute x5, waiting for transfers between devices, swap(): return lax.ppermute(v, axis, [(i, i ^ bit) for i in range(n)])  38.8 us
    ppermute x14, waiting for transfers between devices, shift(): return lax.ppermute(v, axis, [(i, (i + k) % n) for i in range(n)])  33.8 us
    dot_general x2, matrix products, contract(): lax.dot_general(rows, rotated, (((1,), (1,)), ((), ())), precision=lax.Pr...  11 us
  transfers between devices with their start and end apart: 19, of which 7 were waited for; matrix products, arithmetic and copies ran while one was open for 7% of the time, Pallas kernels for 0%

profile of v6, /device:TPU:1, one launch (start us, length us, event | category | flops | bytes accessed | tf_op | source)
XLA Modules:
  0.0 190.1 jit_solution(17187400293941707787)
XLA Ops:
  0.0 3.9 %collective-permute-start.1 = (f32[32,2048]{1,0:T(8,128)}, f32[32,2048]{1,0:T(8,128)S(1)}, u32[]{:S(2)}, u32[]{:S(2)}) collective-permute-start(f32[32,2048]{1,0:T(8,128)} %param.4), channel_id=1, source_target_pairs={{0,16},{16,32},{32,48},{48,0},{1,17},{17,33},{33,49},{49,1},{2,18}... | collective-permute-start | bytes 786440 | tf_op jit(solution)/shard_map/ppermute | solution.py:19
  3.9 15.4 %collective-permute-start.7 = (f32[32,2048]{1,0:T(8,128)}, f32[32,2048]{1,0:T(8,128)S(1)}, u32[]{:S(2)}, u32[]{:S(2)}) collective-permute-start(f32[32,2048]{1,0:T(8,128)} %param.4), channel_id=1, source_target_pairs={{0,64},{64,0},{1,65},{65,1},{2,66},{66,2},{3,67},{67,3},{4,68},{68... | collective-permute-start | bytes 786440 | tf_op jit(solution)/shard_map/ppermute | solution.py:43
  19.4 3.4 %collective-permute-start = (f32[32,2048]{1,0:T(8,128)}, f32[32,2048]{1,0:T(8,128)S(1)}, u32[]{:S(2)}, u32[]{:S(2)}) collective-permute-start(f32[32,2048]{1,0:T(8,128)} %param.4), channel_id=1, source_target_pairs={{0,48},{16,0},{32,16},{48,32},{1,49},{17,1},{33,17},{49,33},{2,50}... | collective-permute-start | bytes 786440 | tf_op jit(solution)/shard_map/ppermute | solution.py:19
  22.8 1.9 %collective-permute-start.2 = (f32[32,2048]{1,0:T(8,128)S(1)}, f32[32,2048]{1,0:T(8,128)S(1)}, u32[]{:S(2)}, u32[]{:S(2)}) collective-permute-start(f32[32,2048]{1,0:T(8,128)S(1)} %collective-permute-done.1), channel_id=1, source_target_pairs={{0,16},{16,32},{32,48},{48,0},{1,17},{17,33},{33,49},{49,1},{2,18}... | collective-permute-start | bytes 786440 | tf_op jit(solution)/shard_map/ppermute | solution.py:19
  24.7 3.8 %collective-permute-start.9 = (f32[32,2048]{1,0:T(8,128)S(1)}, f32[32,2048]{1,0:T(8,128)S(1)}, u32[]{:S(2)}, u32[]{:S(2)}) collective-permute-start(f32[32,2048]{1,0:T(8,128)S(1)} %collective-permute-done.7), channel_id=1, source_target_pairs={{0,128},{128,256},{256,384},{384,0},{1,129},{129,257},{257,385},{3... | collective-permute-start | bytes 786440 | tf_op jit(solution)/shard_map/ppermute | solution.py:19
  28.5 0.0 collective-permute-done
  28.5 3.7 %collective-permute-done.2 = f32[32,2048]{1,0:T(8,128)S(1)} collective-permute-done((f32[32,2048]{1,0:T(8,128)S(1)}, f32[32,2048]{1,0:T(8,128)S(1)}, u32[]{:S(2)}, u32[]{:S(2)}) %collective-permute-start.2) | collective-permute-done | bytes 262176 | tf_op jit(solution)/shard_map/ppermute | solution.py:19
  32.2 1.2 fusion.37
  33.4 3.2 %collective-permute-start.4 = (f32[4,32,2048]{2,1,0:T(8,128)S(1)}, f32[4,32,2048]{2,1,0:T(8,128)S(1)}, u32[]{:S(2)}, u32[]{:S(2)}) collective-permute-start(f32[4,32,2048]{2,1,0:T(8,128)S(1)} %get-tuple-element.8), channel_id=1, source_target_pairs={{0,128},{128,256},{256,384},{384,0},{1,129},{129,257},{257,385},{3... | collective-permute-start | bytes 3145736 | tf_op jit(solution)/shard_map/ppermute | solution.py:19
  36.6 3.4 %collective-permute-start.3 = (f32[4,32,2048]{2,1,0:T(8,128)S(1)}, f32[4,32,2048]{2,1,0:T(8,128)S(1)}, u32[]{:S(2)}, u32[]{:S(2)}) collective-permute-start(f32[4,32,2048]{2,1,0:T(8,128)S(1)} %get-tuple-element.8), channel_id=1, source_target_pairs={{0,384},{128,0},{256,128},{384,256},{1,385},{129,1},{257,129},{385... | collective-permute-start | bytes 3145736 | tf_op jit(solution)/shard_map/ppermute | solution.py:19
  40.0 3.4 %collective-permute-start.8 = (f32[32,2048]{1,0:T(8,128)S(1)}, f32[32,2048]{1,0:T(8,128)S(1)}, u32[]{:S(2)}, u32[]{:S(2)}) collective-permute-start(f32[32,2048]{1,0:T(8,128)S(1)} %collective-permute-done.7), channel_id=1, source_target_pairs={{0,384},{128,0},{256,128},{384,256},{1,385},{129,1},{257,129},{385... | collective-permute-start | bytes 786440 | tf_op jit(solution)/shard_map/ppermute | solution.py:19
  43.4 1.9 %collective-permute-start.10 = (f32[32,2048]{1,0:T(8,128)S(1)}, f32[32,2048]{1,0:T(8,128)S(1)}, u32[]{:S(2)}, u32[]{:S(2)}) collective-permute-start(f32[32,2048]{1,0:T(8,128)S(1)} %collective-permute-done.9), channel_id=1, source_target_pairs={{0,128},{128,256},{256,384},{384,0},{1,129},{129,257},{257,385},{3... | collective-permute-start | bytes 786440 | tf_op jit(solution)/shard_map/ppermute | solution.py:19
  45.3 20.9 %collective-permute-done.8 = f32[32,2048]{1,0:T(8,128)S(1)} collective-permute-done((f32[32,2048]{1,0:T(8,128)S(1)}, f32[32,2048]{1,0:T(8,128)S(1)}, u32[]{:S(2)}, u32[]{:S(2)}) %collective-permute-start.8) | collective-permute-done | bytes 262176 | tf_op jit(solution)/shard_map/ppermute | solution.py:19
  66.2 0.2 fusion.36
  66.5 1.9 %collective-permute-start.12 = (f32[4,32,2048]{2,1,0:T(8,128)S(1)}, f32[4,32,2048]{2,1,0:T(8,128)}, u32[]{:S(2)}, u32[]{:S(2)}) collective-permute-start(f32[4,32,2048]{2,1,0:T(8,128)S(1)} %get-tuple-element.6), channel_id=1, source_target_pairs={{0,16},{16,32},{32,48},{48,0},{1,17},{17,33},{33,49},{49,1},{2,18}... | collective-permute-start | bytes 3145736 | tf_op jit(solution)/shard_map/ppermute | solution.py:19
  68.4 4.6 %collective-permute-start.11 = (f32[4,32,2048]{2,1,0:T(8,128)S(1)}, f32[4,32,2048]{2,1,0:T(8,128)}, u32[]{:S(2)}, u32[]{:S(2)}) collective-permute-start(f32[4,32,2048]{2,1,0:T(8,128)S(1)} %get-tuple-element.6), channel_id=1, source_target_pairs={{0,48},{16,0},{32,16},{48,32},{1,49},{17,1},{33,17},{49,33},{2,50}... | collective-permute-start | bytes 3145736 | tf_op jit(solution)/shard_map/ppermute | solution.py:19
  73.0 0.9 slice.16
  73.9 3.2 %collective-permute-start.5 = (f32[4,16,2048]{2,1,0:T(8,128)}, f32[4,16,2048]{2,1,0:T(8,128)}, u32[]{:S(2)}, u32[]{:S(2)}) collective-permute-start(f32[4,16,2048]{2,1,0:T(8,128)} %slice.16), channel_id=1, source_target_pairs={{0,128},{128,256},{256,384},{384,0},{1,129},{129,257},{257,385},{3... | collective-permute-start | bytes 1572872 | tf_op jit(solution)/shard_map/ppermute | solution.py:19
  77.1 0.9 slice.17
  78.0 0.2 copy-done.2
  78.2 3.3 %collective-permute-start.6 = (f32[4,16,2048]{2,1,0:T(8,128)}, f32[4,16,2048]{2,1,0:T(8,128)}, u32[]{:S(2)}, u32[]{:S(2)}) collective-permute-start(f32[4,16,2048]{2,1,0:T(8,128)} %slice.17), channel_id=1, source_target_pairs={{0,384},{128,0},{256,128},{384,256},{1,385},{129,1},{257,129},{385... | collective-permute-start | bytes 1572872 | tf_op jit(solution)/shard_map/ppermute | solution.py:19
  81.7 9.2 %collective-permute-done.12 = f32[4,32,2048]{2,1,0:T(8,128)} collective-permute-done((f32[4,32,2048]{2,1,0:T(8,128)S(1)}, f32[4,32,2048]{2,1,0:T(8,128)}, u32[]{:S(2)}, u32[]{:S(2)}) %collective-permute-start.12) | collective-permute-done | bytes 1048608 | tf_op jit(solution)/shard_map/ppermute | solution.py:19
  90.9 1.1 slice.18
  92.0 1.9 %collective-permute-start.13 = (f32[4,16,2048]{2,1,0:T(8,128)S(1)}, f32[4,16,2048]{2,1,0:T(8,128)S(1)}, u32[]{:S(2)}, u32[]{:S(2)}) collective-permute-start(f32[4,16,2048]{2,1,0:T(8,128)S(1)} %slice.18), channel_id=1, source_target_pairs={{0,16},{16,32},{32,48},{48,0},{1,17},{17,33},{33,49},{49,1},{2,18}... | collective-permute-start | bytes 1572872 | tf_op jit(solution)/shard_map/ppermute | solution.py:19
  93.9 1.1 slice.19
  95.0 4.6 %collective-permute-start.14 = (f32[4,16,2048]{2,1,0:T(8,128)S(1)}, f32[4,16,2048]{2,1,0:T(8,128)S(1)}, u32[]{:S(2)}, u32[]{:S(2)}) collective-permute-start(f32[4,16,2048]{2,1,0:T(8,128)S(1)} %slice.19), channel_id=1, source_target_pairs={{0,48},{16,0},{32,16},{48,32},{1,49},{17,1},{33,17},{49,33},{2,50}... | collective-permute-start | bytes 1572872 | tf_op jit(solution)/shard_map/ppermute | solution.py:19
  99.6 1.3 maximum_bitcast_fusion
  100.9 0.0 copy-start.5
  100.9 6.0 %fusion.29 = f32[4,4,1,32,512]{4,3,1,0,2:T(8,128)S(1)} fusion(f32[512,2048]{1,0:T(8,128)} %param.3, f32[1,4,32,2048]{3,2,1,0:T(8,128)S(1)} %bitcast.76, f32[1,4,32,2048]{3,2,1,0:T(8,128)S(1)} %maximum_bitcast_fusion, f32[1,4,32,2048]{3,2,1,0:T(8,128)S(1)} %bitcast.77, f32[1,4,32,2048]{3,2,1,0:T(8,128)S(1)} %get-tuple-element.7), kind=kOutput, calls=%fused_computation.33 | convolution fusion | flops 3224371200 | bytes 9437184 | tf_op jit(solution)/shard_map/dot_general | solution.py:13
  106.9 0.1 maximum_bitcast_fusion.1
  107.0 5.0 %fusion.24 = f32[4,4,1,32,512]{4,3,1,0,2:T(8,128)S(1)} fusion(f32[512,2048]{1,0:T(8,128)S(1)} %copy-done.5, f32[1,4,32,2048]{3,2,0,1:T(8,128)} %bitcast.21, f32[1,4,32,2048]{3,2,0,1:T(8,128)S(1)} %maximum_bitcast_fusion.1, f32[1,4,32,2048]{3,2,0,1:T(8,128)} %bitcast.18, f32[1,4,32,2048]{3,2,0,1:T(8,128)S(1)} %get-tuple-element.5), kind=kOutput, calls=%fused_computation.32 | convolution fusion | flops 3224371200 | bytes 9437184 | tf_op jit(solution)/shard_map/dot_general | solution.py:13
  112.1 0.5 fusion.23
  112.6 0.5 fusion.20
  113.1 0.5 fusion.19
  113.7 0.2 copy.10
  113.9 0.1 dynamic-slice_bitcast_fusion
  114.0 0.0 copy-start.4
  114.0 7.0 %collective-permute-start.15 = (f32[8,64,512]{2,1,0:T(8,128)S(1)}, f32[8,64,512]{2,1,0:T(8,128)}, u32[]{:S(2)}, u32[]{:S(2)}) collective-permute-start(f32[8,64,512]{2,1,0:T(8,128)S(1)} %dynamic-slice_bitcast_fusion), channel_id=1, source_target_pairs={{0,1},{1,0},{2,3},{3,2},{4,5},{5,4},{6,7},{7,6},{8,9},{9,8},{10,11... | collective-permute-start | bytes 3145736 | tf_op jit(solution)/shard_map/ppermute | solution.py:43
  121.0 2.4 %collective-permute-done.15 = f32[8,64,512]{2,1,0:T(8,128)} collective-permute-done((f32[8,64,512]{2,1,0:T(8,128)S(1)}, f32[8,64,512]{2,1,0:T(8,128)}, u32[]{:S(2)}, u32[]{:S(2)}) %collective-permute-start.15) | collective-permute-done | bytes 1048608 | tf_op jit(solution)/shard_map/ppermute | solution.py:43
  123.3 1.4 bitcast_add_fusion
  124.8 18.0 %collective-permute-start.16 = (f32[4,64,512]{2,1,0:T(8,128)S(1)}, f32[4,64,512]{2,1,0:T(8,128)S(1)}, u32[]{:S(2)}, u32[]{:S(2)}) collective-permute-start(f32[4,64,512]{2,1,0:T(8,128)S(1)} %dynamic-slice_bitcast_fusion.1), channel_id=1, source_target_pairs={{0,2},{2,0},{4,6},{6,4},{8,10},{10,8},{12,14},{14,12},{1,3},{3,1},... | collective-permute-start | bytes 1572872 | tf_op jit(solution)/shard_map/ppermute | solution.py:43
  142.9 11.9 %collective-permute-done.16 = f32[4,64,512]{2,1,0:T(8,128)S(1)} collective-permute-done((f32[4,64,512]{2,1,0:T(8,128)S(1)}, f32[4,64,512]{2,1,0:T(8,128)S(1)}, u32[]{:S(2)}, u32[]{:S(2)}) %collective-permute-start.16) | collective-permute-done | bytes 524320 | tf_op jit(solution)/shard_map/ppermute | solution.py:43
  154.8 0.1 bitcast_add_fusion.1
  154.9 1.9 %collective-permute-start.17 = (f32[2,64,512]{2,1,0:T(8,128)S(1)}, f32[2,64,512]{2,1,0:T(8,128)S(1)}, u32[]{:S(2)}, u32[]{:S(2)}) collective-permute-start(f32[2,64,512]{2,1,0:T(8,128)S(1)} %dynamic-slice_bitcast_fusion.2), channel_id=1, source_target_pairs={{0,4},{2,6},{4,0},{6,2},{8,12},{10,14},{12,8},{14,10},{1,5},{3,7},... | collective-permute-start | bytes 786440 | tf_op jit(solution)/shard_map/ppermute | solution.py:43
  156.8 13.8 %collective-permute-done.17 = f32[2,64,512]{2,1,0:T(8,128)S(1)} collective-permute-done((f32[2,64,512]{2,1,0:T(8,128)S(1)}, f32[2,64,512]{2,1,0:T(8,128)S(1)}, u32[]{:S(2)}, u32[]{:S(2)}) %collective-permute-start.17) | collective-permute-done | bytes 262176 | tf_op jit(solution)/shard_map/ppermute | solution.py:43
  170.7 8.0 %collective-permute-start.18 = (f32[1,64,512]{2,1,0:T(8,128)S(1)}, f32[1,64,512]{2,1,0:T(8,128)S(1)}, u32[]{:S(2)}, u32[]{:S(2)}) collective-permute-start(f32[1,64,512]{2,1,0:T(8,128)S(1)} %constant_dynamic-slice_fusion), channel_id=1, source_target_pairs={{0,8},{2,10},{4,12},{6,14},{8,0},{10,2},{12,4},{14,6},{1,9},{3,11}... | collective-permute-start | bytes 393224 | tf_op jit(solution)/shard_map/ppermute | solution.py:43
  178.7 10.7 %collective-permute-done.18 = f32[1,64,512]{2,1,0:T(8,128)S(1)} collective-permute-done((f32[1,64,512]{2,1,0:T(8,128)S(1)}, f32[1,64,512]{2,1,0:T(8,128)S(1)}, u32[]{:S(2)}, u32[]{:S(2)}) %collective-permute-start.18) | collective-permute-done | bytes 131104 | tf_op jit(solution)/shard_map/ppermute | solution.py:43
  189.4 0.7 bitcast_subtract_fusion
  (24 shorter events, 0.2 us)
Async XLA Ops:
  0.0 22.8 %collective-permute-start.1 = (f32[32,2048]{1,0:T(8,128)}, f32[32,2048]{1,0:T(8,128)S(1)}, u32[]{:S(2)}, u32[]{:S(2)}) collective-permute-start(f32[32,2048]{1,0:T(8,128)} %param.4), channel_id=1, source_target_pairs={{0,16},{16,32},{32,48},{48,0},{1,17},{17,33},{33,49},{49,1},{2,18}... | collective-permute-start | bytes 786440 | tf_op jit(solution)/shard_map/ppermute | solution.py:19
  3.9 20.8 %collective-permute-start.7 = (f32[32,2048]{1,0:T(8,128)}, f32[32,2048]{1,0:T(8,128)S(1)}, u32[]{:S(2)}, u32[]{:S(2)}) collective-permute-start(f32[32,2048]{1,0:T(8,128)} %param.4), channel_id=1, source_target_pairs={{0,64},{64,0},{1,65},{65,1},{2,66},{66,2},{3,67},{67,3},{4,68},{68... | collective-permute-start | bytes 786440 | tf_op jit(solution)/shard_map/ppermute | solution.py:43
  19.4 9.1 %collective-permute-start = (f32[32,2048]{1,0:T(8,128)}, f32[32,2048]{1,0:T(8,128)S(1)}, u32[]{:S(2)}, u32[]{:S(2)}) collective-permute-start(f32[32,2048]{1,0:T(8,128)} %param.4), channel_id=1, source_target_pairs={{0,48},{16,0},{32,16},{48,32},{1,49},{17,1},{33,17},{49,33},{2,50}... | collective-permute-start | bytes 786440 | tf_op jit(solution)/shard_map/ppermute | solution.py:19
  22.8 9.4 %collective-permute-start.2 = (f32[32,2048]{1,0:T(8,128)S(1)}, f32[32,2048]{1,0:T(8,128)S(1)}, u32[]{:S(2)}, u32[]{:S(2)}) collective-permute-start(f32[32,2048]{1,0:T(8,128)S(1)} %collective-permute-done.1), channel_id=1, source_target_pairs={{0,16},{16,32},{32,48},{48,0},{1,17},{17,33},{33,49},{49,1},{2,18}... | collective-permute-start | bytes 786440 | tf_op jit(solution)/shard_map/ppermute | solution.py:19
  24.7 18.7 %collective-permute-start.9 = (f32[32,2048]{1,0:T(8,128)S(1)}, f32[32,2048]{1,0:T(8,128)S(1)}, u32[]{:S(2)}, u32[]{:S(2)}) collective-permute-start(f32[32,2048]{1,0:T(8,128)S(1)} %collective-permute-done.7), channel_id=1, source_target_pairs={{0,128},{128,256},{256,384},{384,0},{1,129},{129,257},{257,385},{3... | collective-permute-start | bytes 786440 | tf_op jit(solution)/shard_map/ppermute | solution.py:19
  33.4 39.5 %collective-permute-start.4 = (f32[4,32,2048]{2,1,0:T(8,128)S(1)}, f32[4,32,2048]{2,1,0:T(8,128)S(1)}, u32[]{:S(2)}, u32[]{:S(2)}) collective-permute-start(f32[4,32,2048]{2,1,0:T(8,128)S(1)} %get-tuple-element.8), channel_id=1, source_target_pairs={{0,128},{128,256},{256,384},{384,0},{1,129},{129,257},{257,385},{3... | collective-permute-start | bytes 3145736 | tf_op jit(solution)/shard_map/ppermute | solution.py:19
  36.6 40.4 %collective-permute-start.3 = (f32[4,32,2048]{2,1,0:T(8,128)S(1)}, f32[4,32,2048]{2,1,0:T(8,128)S(1)}, u32[]{:S(2)}, u32[]{:S(2)}) collective-permute-start(f32[4,32,2048]{2,1,0:T(8,128)S(1)} %get-tuple-element.8), channel_id=1, source_target_pairs={{0,384},{128,0},{256,128},{384,256},{1,385},{129,1},{257,129},{385... | collective-permute-start | bytes 3145736 | tf_op jit(solution)/shard_map/ppermute | solution.py:19
  40.0 26.2 %collective-permute-start.8 = (f32[32,2048]{1,0:T(8,128)S(1)}, f32[32,2048]{1,0:T(8,128)S(1)}, u32[]{:S(2)}, u32[]{:S(2)}) collective-permute-start(f32[32,2048]{1,0:T(8,128)S(1)} %collective-permute-done.7), channel_id=1, source_target_pairs={{0,384},{128,0},{256,128},{384,256},{1,385},{129,1},{257,129},{385... | collective-permute-start | bytes 786440 | tf_op jit(solution)/shard_map/ppermute | solution.py:19
  43.4 22.8 %collective-permute-start.10 = (f32[32,2048]{1,0:T(8,128)S(1)}, f32[32,2048]{1,0:T(8,128)S(1)}, u32[]{:S(2)}, u32[]{:S(2)}) collective-permute-start(f32[32,2048]{1,0:T(8,128)S(1)} %collective-permute-done.9), channel_id=1, source_target_pairs={{0,128},{128,256},{256,384},{384,0},{1,129},{129,257},{257,385},{3... | collective-permute-start | bytes 786440 | tf_op jit(solution)/shard_map/ppermute | solution.py:19
  66.5 24.4 %collective-permute-start.12 = (f32[4,32,2048]{2,1,0:T(8,128)S(1)}, f32[4,32,2048]{2,1,0:T(8,128)}, u32[]{:S(2)}, u32[]{:S(2)}) collective-permute-start(f32[4,32,2048]{2,1,0:T(8,128)S(1)} %get-tuple-element.6), channel_id=1, source_target_pairs={{0,16},{16,32},{32,48},{48,0},{1,17},{17,33},{33,49},{49,1},{2,18}... | collective-permute-start | bytes 3145736 | tf_op jit(solution)/shard_map/ppermute | solution.py:19
  68.4 25.5 %collective-permute-start.11 = (f32[4,32,2048]{2,1,0:T(8,128)S(1)}, f32[4,32,2048]{2,1,0:T(8,128)}, u32[]{:S(2)}, u32[]{:S(2)}) collective-permute-start(f32[4,32,2048]{2,1,0:T(8,128)S(1)} %get-tuple-element.6), channel_id=1, source_target_pairs={{0,48},{16,0},{32,16},{48,32},{1,49},{17,1},{33,17},{49,33},{2,50}... | collective-permute-start | bytes 3145736 | tf_op jit(solution)/shard_map/ppermute | solution.py:19
  73.0 4.1 %copy-start = (f32[4,32,2048]{2,1,0:T(8,128)}, f32[4,32,2048]{2,1,0:T(8,128)S(1)}, u32[]{:S(2)}) copy-start(f32[4,32,2048]{2,1,0:T(8,128)S(1)} %collective-permute-done.4) | copy-start | bytes 3145732
  73.9 25.7 %collective-permute-start.5 = (f32[4,16,2048]{2,1,0:T(8,128)}, f32[4,16,2048]{2,1,0:T(8,128)}, u32[]{:S(2)}, u32[]{:S(2)}) collective-permute-start(f32[4,16,2048]{2,1,0:T(8,128)} %slice.16), channel_id=1, source_target_pairs={{0,128},{128,256},{256,384},{384,0},{1,129},{129,257},{257,385},{3... | collective-permute-start | bytes 1572872 | tf_op jit(solution)/shard_map/ppermute | solution.py:19
  77.1 1.1 copy-start.2
  78.2 21.3 %collective-permute-start.6 = (f32[4,16,2048]{2,1,0:T(8,128)}, f32[4,16,2048]{2,1,0:T(8,128)}, u32[]{:S(2)}, u32[]{:S(2)}) collective-permute-start(f32[4,16,2048]{2,1,0:T(8,128)} %slice.17), channel_id=1, source_target_pairs={{0,384},{128,0},{256,128},{384,256},{1,385},{129,1},{257,129},{385... | collective-permute-start | bytes 1572872 | tf_op jit(solution)/shard_map/ppermute | solution.py:19
  81.6 19.3 %copy-start.1 = (f32[4,32,2048]{2,1,0:T(8,128)S(1)}, f32[4,32,2048]{2,1,0:T(8,128)}, u32[]{:S(2)}) copy-start(f32[4,32,2048]{2,1,0:T(8,128)} %copy-done) | copy-start | bytes 3145732
  81.6 19.3 %copy-start.3 = (f32[4,32,2048]{2,1,0:T(8,128)S(1)}, f32[4,32,2048]{2,1,0:T(8,128)}, u32[]{:S(2)}) copy-start(f32[4,32,2048]{2,1,0:T(8,128)} %copy-done.2) | copy-start | bytes 3145732
  92.0 15.0 %collective-permute-start.13 = (f32[4,16,2048]{2,1,0:T(8,128)S(1)}, f32[4,16,2048]{2,1,0:T(8,128)S(1)}, u32[]{:S(2)}, u32[]{:S(2)}) collective-permute-start(f32[4,16,2048]{2,1,0:T(8,128)S(1)} %slice.18), channel_id=1, source_target_pairs={{0,16},{16,32},{32,48},{48,0},{1,17},{17,33},{33,49},{49,1},{2,18}... | collective-permute-start | bytes 1572872 | tf_op jit(solution)/shard_map/ppermute | solution.py:19
  95.0 11.9 %collective-permute-start.14 = (f32[4,16,2048]{2,1,0:T(8,128)S(1)}, f32[4,16,2048]{2,1,0:T(8,128)S(1)}, u32[]{:S(2)}, u32[]{:S(2)}) collective-permute-start(f32[4,16,2048]{2,1,0:T(8,128)S(1)} %slice.19), channel_id=1, source_target_pairs={{0,48},{16,0},{32,16},{48,32},{1,49},{17,1},{33,17},{49,33},{2,50}... | collective-permute-start | bytes 1572872 | tf_op jit(solution)/shard_map/ppermute | solution.py:19
  100.9 6.1 %copy-start.5 = (f32[512,2048]{1,0:T(8,128)S(1)}, f32[512,2048]{1,0:T(8,128)}, u32[]{:S(2)}) copy-start(f32[512,2048]{1,0:T(8,128)} %param.3) | copy-start | bytes 12582916
  114.0 75.4 %copy-start.4 = (f32[64,512]{1,0:T(8,128)S(1)}, f32[64,512]{1,0:T(8,128)}, u32[]{:S(2)}) copy-start(f32[64,512]{1,0:T(8,128)} %param.5) | copy-start | bytes 393220
  114.0 9.4 %collective-permute-start.15 = (f32[8,64,512]{2,1,0:T(8,128)S(1)}, f32[8,64,512]{2,1,0:T(8,128)}, u32[]{:S(2)}, u32[]{:S(2)}) collective-permute-start(f32[8,64,512]{2,1,0:T(8,128)S(1)} %dynamic-slice_bitcast_fusion), channel_id=1, source_target_pairs={{0,1},{1,0},{2,3},{3,2},{4,5},{5,4},{6,7},{7,6},{8,9},{9,8},{10,11... | collective-permute-start | bytes 3145736 | tf_op jit(solution)/shard_map/ppermute | solution.py:43
  124.8 29.9 %collective-permute-start.16 = (f32[4,64,512]{2,1,0:T(8,128)S(1)}, f32[4,64,512]{2,1,0:T(8,128)S(1)}, u32[]{:S(2)}, u32[]{:S(2)}) collective-permute-start(f32[4,64,512]{2,1,0:T(8,128)S(1)} %dynamic-slice_bitcast_fusion.1), channel_id=1, source_target_pairs={{0,2},{2,0},{4,6},{6,4},{8,10},{10,8},{12,14},{14,12},{1,3},{3,1},... | collective-permute-start | bytes 1572872 | tf_op jit(solution)/shard_map/ppermute | solution.py:43
  154.9 15.7 %collective-permute-start.17 = (f32[2,64,512]{2,1,0:T(8,128)S(1)}, f32[2,64,512]{2,1,0:T(8,128)S(1)}, u32[]{:S(2)}, u32[]{:S(2)}) collective-permute-start(f32[2,64,512]{2,1,0:T(8,128)S(1)} %dynamic-slice_bitcast_fusion.2), channel_id=1, source_target_pairs={{0,4},{2,6},{4,0},{6,2},{8,12},{10,14},{12,8},{14,10},{1,5},{3,7},... | collective-permute-start | bytes 786440 | tf_op jit(solution)/shard_map/ppermute | solution.py:43
  170.7 18.7 %collective-permute-start.18 = (f32[1,64,512]{2,1,0:T(8,128)S(1)}, f32[1,64,512]{2,1,0:T(8,128)S(1)}, u32[]{:S(2)}, u32[]{:S(2)}) collective-permute-start(f32[1,64,512]{2,1,0:T(8,128)S(1)} %constant_dynamic-slice_fusion), channel_id=1, source_target_pairs={{0,8},{2,10},{4,12},{6,14},{8,0},{10,2},{12,4},{14,6},{1,9},{3,11}... | collective-permute-start | bytes 393224 | tf_op jit(solution)/shard_map/ppermute | solution.py:43
